TPU v7x, 256 devices: a whole 4x4x8 slice. The times are simulated.
256 devices in a mesh: grp: 4 (over y), mdl: 64 (over z, x, core).
Axes of the slice: x: 4, y: 4, z: 8, core: 2. Of those that a mesh axis runs over, the one named last changes fastest.
Arguments:
- pol_hidden: bfloat16 [1024, 4096], P(('grp', 'mdl')), may hold values from -6 to 6
- ref_hidden: bfloat16 [1024, 4096], P(('grp', 'mdl')), may hold values from -6 to 6
- pol_mlp_gain: bfloat16 [4096], replicated, may hold values from 0.099609375 to 1.8984375
- ref_mlp_gain: bfloat16 [4096], replicated, may hold values from 0.099609375 to 1.8984375
- pol_final_gain: bfloat16 [4096], replicated, may hold values from 0.099609375 to 1.8984375
- ref_final_gain: bfloat16 [4096], replicated, may hold values from 0.099609375 to 1.8984375
- pol_gate: bfloat16 [4096, 11008], P(None, 'mdl'), may hold values from -0.09375 to 0.09375
- pol_up: bfloat16 [4096, 11008], P(None, 'mdl'), may hold values from -0.09375 to 0.09375
- pol_down: bfloat16 [11008, 4096], P('mdl'), may hold values from -0.109375 to 0.109375
- ref_gate: bfloat16 [4096, 11008], P(None, 'mdl'), may hold values from -0.09375 to 0.09375
- ref_up: bfloat16 [4096, 11008], P(None, 'mdl'), may hold values from -0.09375 to 0.09375
- ref_down: bfloat16 [11008, 4096], P('mdl'), may hold values from -0.109375 to 0.109375
- pol_head: bfloat16 [64000, 4096], P(('grp', 'mdl')), may hold values from -20 to 20
- ref_head: bfloat16 [64000, 4096], P(('grp', 'mdl')), may hold values from -20 to 20
- token_ids: int32 [1024], replicated, may hold values from 0 to 63999
- lengths: int32 [16], replicated, may hold values from 1 to 160, 1024 in all
Outputs:
- pol_out: bfloat16 [1024, 4096], P(('grp', 'mdl'))
- ref_out: bfloat16 [1024, 4096], P(('grp', 'mdl'))
- rollout_ratio: float32 [16], replicated
Inputs may be any that keep to these rules, and one draw needn't show every extreme that they name: Rollout lengths sum to 1024; the longest is exactly 160.
All inputs are finite; a program needn't handle non-finite values.
Results may differ from a plain program's by a relative error of at most 0.012.
The roundings to bfloat16 on the way count: a program that leaves them out, or rounds other values in their place, can miss the bound.
Values may be sent and summed in bfloat16 or wider, within the bound.
No kernel may reach another device: no remote copies, remote signals or barrier semaphores. Data moves between devices by JAX's collectives and lax.ppermute only.
A program may use at most 128 MiB of HBM per device.

v0:
```python
import jax
import jax.numpy as jnp
from jax import lax
from jax.sharding import Mesh
from jax.sharding import PartitionSpec as P

SWAP = [(0, 1), (1, 0)]


def rms_rows(rows, gain):
    values = rows.astype(jnp.float32)
    scale = lax.rsqrt(jnp.mean(values * values, axis=-1, keepdims=True) + 1e-05)
    return (values * scale * gain.astype(jnp.float32)).astype(jnp.bfloat16)


def mlp_partial(piece, gain, w_gate, w_up, w_down):
    normed = rms_rows(piece, gain)
    gate = jnp.dot(normed, w_gate, preferred_element_type=jnp.float32)
    upper = jnp.dot(normed, w_up, preferred_element_type=jnp.float32)
    hidden = (jax.nn.silu(gate) * upper).astype(jnp.bfloat16)
    return jnp.dot(hidden, w_down, preferred_element_type=jnp.float32)


def vocab_terms(token_rows, head_rows, targets, vocab):
    logits = jnp.einsum("td,vd->tv", token_rows, head_rows, preferred_element_type=jnp.float32)
    peak = jnp.max(logits, axis=1)
    total = jnp.sum(jnp.exp(logits - peak[:, None]), axis=1)
    target = jnp.sum(jnp.where(targets[:, None] == vocab[None, :], logits, 0.0), axis=1)
    return (peak, total, target)


def merge_terms(lo, hi):
    peak = jnp.maximum(lo[:, 0], hi[:, 0])
    total = lo[:, 1] * jnp.exp(lo[:, 0] - peak) + hi[:, 1] * jnp.exp(hi[:, 0] - peak)
    return jnp.stack([peak, total, lo[:, 2] + hi[:, 2]], axis=1)


def rollout_totals(log_ratio, positions, lengths):
    ends = jnp.cumsum(lengths)
    owner = jnp.sum((positions[:, None] >= ends[None, :]).astype(jnp.int32), axis=1)
    onehot = (owner[:, None] == jnp.arange(lengths.shape[0], dtype=jnp.int32)[None, :]).astype(
        jnp.float32
    )
    return jnp.sum(log_ratio[:, None] * onehot, axis=0)


def zx_bits():
    size = lax.axis_size("zx")
    return [1 << k for k in reversed(range(size.bit_length() - 1))]


def partner_mask(bit):
    return 3 if bit == 2 else bit


def gather_doubling(block, orders=((16, 8, 1, 4, 2), (16, 1, 8, 2, 4))):
    bits = zx_bits()
    spot = lax.axis_index("zx")
    size = lax.axis_size("zx")
    width = block.shape[-1] // len(orders)
    parts = []
    for k in range(len(orders)):
        piece = lax.slice_in_dim(block, k * width, (k + 1) * width, axis=block.ndim - 1)
        parts.append(piece.reshape((1,) * len(bits) + piece.shape))
    for step in range(len(orders[0])):
        for k, order in enumerate(orders):
            bit = order[step]
            if bit not in bits:
                continue
            dim = bits.index(bit)
            held = parts[k]
            other = lax.ppermute(held, "zx", [(i, i ^ partner_mask(bit)) for i in range(size)])
            low = (spot & bit) == 0
            parts[k] = jnp.concatenate(
                [jnp.where(low, held, other), jnp.where(low, other, held)], axis=dim
            )
    rows = [p.reshape((-1,) + p.shape[len(bits) + 1 :]) for p in parts]
    return jnp.concatenate(rows, axis=-1)


def scatter_halving(full, orders=((2, 4, 1, 8, 16), (4, 2, 8, 1, 16))):
    bits = zx_bits()
    spot = lax.axis_index("zx")
    size = lax.axis_size("zx")
    width = full.shape[-1] // len(orders)
    parts = []
    for k in range(len(orders)):
        piece = lax.slice_in_dim(full, k * width, (k + 1) * width, axis=full.ndim - 1)
        parts.append(piece.reshape((2,) * len(bits) + (-1,) + piece.shape[1:]))
    for step in range(len(orders[0])):
        for k, order in enumerate(orders):
            bit = order[step]
            if bit not in bits:
                continue
            dim = bits.index(bit)
            held = parts[k]
            lower = lax.slice_in_dim(held, 0, 1, axis=dim)
            upper = lax.slice_in_dim(held, 1, 2, axis=dim)
            low = (spot & bit) == 0
            other = lax.ppermute(
                jnp.where(low, upper, lower), "zx", [(i, i ^ partner_mask(bit)) for i in range(size)]
            )
            parts[k] = jnp.where(low, lower, upper) + other
    rows = [p.reshape((-1,) + full.shape[1:-1] + (width,)) for p in parts]
    return jnp.concatenate(rows, axis=-1)


def pick(first, pol, ref):
    return jnp.where(first, pol, ref), jnp.where(first, ref, pol)


def per_device(
    pol_hidden,
    ref_hidden,
    pol_mlp_gain,
    ref_mlp_gain,
    pol_final_gain,
    ref_final_gain,
    pol_gate,
    pol_up,
    pol_down,
    ref_gate,
    ref_up,
    ref_down,
    pol_head,
    ref_head,
    token_ids,
    lengths,
):
    rows = pol_hidden.shape[0]
    core = lax.axis_index("core")
    spot = lax.axis_index("zx")
    group = lax.axis_index("grp")
    first = core == 0
    per_group = lax.axis_size("zx") * 2
    member = spot * 2 + core
    partner = spot * 2 + (1 - core)

    pol_w = (pol_gate, pol_up, pol_down)
    ref_w = (ref_gate, ref_up, ref_down)
    got_w = lax.ppermute(lax.cond(first, lambda: ref_w, lambda: pol_w), "core", SWAP)
    keep_h, give_h = pick(first, pol_hidden, ref_hidden)
    got_h = lax.ppermute(give_h, "core", SWAP)
    pair_rows = jnp.where(
        first, jnp.concatenate([keep_h, got_h]), jnp.concatenate([got_h, keep_h])
    )
    group_rows = gather_doubling(pair_rows)
    mlp_gain = jnp.where(first, pol_mlp_gain, ref_mlp_gain)
    units = pol_gate.shape[1]
    gate_up = jnp.concatenate(
        [jnp.where(first, pol_gate, ref_gate), got_w[0], jnp.where(first, pol_up, ref_up), got_w[1]],
        axis=1,
    )
    down = jnp.concatenate([jnp.where(first, pol_down, ref_down), got_w[2]], axis=0)
    normed = rms_rows(group_rows, mlp_gain)
    both = jnp.dot(normed, gate_up, preferred_element_type=jnp.float32)
    gate, upper = both[:, : 2 * units], both[:, 2 * units :]
    hidden = (jax.nn.silu(gate) * upper).astype(jnp.bfloat16)
    partial = jnp.dot(hidden, down, preferred_element_type=jnp.float32)
    mixed = scatter_halving(partial)
    out = (pair_rows.astype(jnp.float32) + mixed).astype(jnp.bfloat16)
    final = gather_doubling(rms_rows(out, jnp.where(first, pol_final_gain, ref_final_gain)))
    mine_out = lax.dynamic_slice_in_dim(out, core * rows, rows, axis=0)
    sent_out = lax.ppermute(lax.dynamic_slice_in_dim(out, (1 - core) * rows, rows, axis=0), "core", SWAP)
    pol_out = jnp.where(first, mine_out, sent_out)
    ref_out = jnp.where(first, sent_out, mine_out)

    every = lax.all_gather(final, "grp", axis=0, tiled=True)
    keep_v, give_v = pick(first, pol_head, ref_head)
    got_v = lax.ppermute(give_v, "core", SWAP)
    voc_dev = pol_head.shape[0]
    positions = jnp.arange(every.shape[0], dtype=jnp.int32)
    base = group * per_group
    vocab = jnp.concatenate(
        [
            (base + member) * voc_dev + jnp.arange(voc_dev, dtype=jnp.int32),
            (base + partner) * voc_dev + jnp.arange(voc_dev, dtype=jnp.int32),
        ]
    )
    own_terms = jnp.stack(vocab_terms(every, jnp.concatenate([keep_v, got_v]), token_ids, vocab))
    other_terms = lax.ppermute(own_terms, "core", SWAP)
    state = jnp.where(first, jnp.stack([own_terms, other_terms]), jnp.stack([other_terms, own_terms]))
    rounds = [("zx", 1), ("zx", 2), ("zx", 4), ("zx", 8), ("zx", 16), ("grp", 1), ("grp", 2)]
    for axis, bit in rounds:
        size = lax.axis_size(axis)
        other = lax.ppermute(state, axis, [(i, i ^ partner_mask(bit)) for i in range(size)])
        low = (lax.axis_index(axis) & bit) == 0
        state = merge_terms(jnp.where(low, state, other), jnp.where(low, other, state))
    logp = state[:, 2] - state[:, 0] - jnp.log(state[:, 1])
    rollout_ratio = rollout_totals(logp[0] - logp[1], positions, lengths)
    return (pol_out, ref_out, rollout_ratio)


def solution(mesh):
    groups, members = mesh.devices.shape
    split = Mesh(mesh.devices.reshape(groups, members // 2, 2), ("grp", "zx", "core"))
    rows = P(("grp", "zx", "core"), None)
    units = ("zx", "core")
    placed = (
        rows,
        rows,
        P(),
        P(),
        P(),
        P(),
        P(None, units),
        P(None, units),
        P(units, None),
        P(None, units),
        P(None, units),
        P(units, None),
        rows,
        rows,
        P(),
        P(),
    )
    return jax.shard_map(
        per_device,
        mesh=split,
        in_specs=placed,
        out_specs=(rows, rows, P()),
        check_vma=False,
    )
```

profile of v0, /device:TPU:6, one launch (start us, length us, event | category | flops | bytes accessed | tf_op | source)
XLA Modules:
  0.0 322.0 jit_solution(18077545841143333423)
XLA Ops:
  8.1 4.3 %conditional.1 = (bf16[172,4096]{1,0:T(8,128)(2,1)S(1)}, bf16[4096,172]{0,1:T(8,128)(2,1)}, bf16[4096,172]{0,1:T(8,128)(2,1)}) conditional(s32[]{:T(128)} %convert_element_type.38, (bf16[4096,172]{0,1:T(8,128)(2,1)}, bf16[4096,172]{0,1:T(8,128)(2,1)}, bf16[172,4096]{1,0:T(8,128)(2,1)}) %tuple.14, (bf16[4096,172]{0,1:T(8,128)(2,1)}, ...), branch_computations={%region_1.0_spmd, %region_2.3_spmd} | conditional | bytes 19726416 | solution.py:141
  13.4 3.9 %broadcast_select_fusion.3 = (bf16[4096,172]{0,1:T(8,128)(2,1)}, bf16[4096,172]{0,1:T(8,128)(2,1)}) fusion(bf16[4096,172]{0,1:T(8,128)(2,1)} %param.25, bf16[4096,172]{0,1:T(8,128)(2,1)} %param.28, pred[]{:T(512)S(6)} %eq.28, bf16[4096,172]{0,1:T(8,128)(2,1)} %param.24, bf16[4096,172]{0,1:T(8,128)(2,1)} %param.27), kind=kLoop, calls=%fused_computation.30 | loop fusion | flops 1409024 | bytes 8454145 | tf_op jit(solution)/shard_map/jit(_where)/select_n | solution.py:151
  17.4 7.3 %collective-permute-start.1 = (bf16[1,1,1,1,1,8,2048]{6,5,4,3,2,1,0:T(8,128)(2,1)S(1)}, bf16[1,1,1,1,1,8,2048]{6,5,4,3,2,1,0:T(8,128)(2,1)S(1)}, u32[]{:S(2)}, u32[]{:S(2)}) collective-permute-start(bf16[1,1,1,1,1,8,2048]{6,5,4,3,2,1,0:T(8,128)(2,1)S(1)} %get-tuple-element.115), channel_id=1, source_target_pairs={{0,32},{2,34},{4,36},{6,38},{8,40},{10,42},{12,44},{14,46},{16,48}... | collective-permute-start | bytes 98312 | tf_op jit(solution)/shard_map/ppermute | solution.py:72
  26.6 6.3 %collective-permute-done.6 = bf16[1,1,1,1,1,8,2048]{6,5,4,3,2,1,0:T(8,128)(2,1)S(1)} collective-permute-done((bf16[1,1,1,1,1,8,2048]{6,5,4,3,2,1,0:T(8,128)(2,1)S(1)}, bf16[1,1,1,1,1,8,2048]{6,5,4,3,2,1,0:T(8,128)(2,1)S(1)}, u32[]{:S(2)}, u32[]{:S(2)}) %collective-permute-start.6) | collective-permute-done | bytes 32800 | tf_op jit(solution)/shard_map/ppermute | solution.py:72
  35.2 3.6 %collective-permute-done.2 = bf16[2,1,1,1,1,8,2048]{6,5,4,3,2,1,0:T(8,128)(2,1)S(1)} collective-permute-done((bf16[2,1,1,1,1,8,2048]{6,5,4,3,2,1,0:T(8,128)(2,1)S(1)}, bf16[2,1,1,1,1,8,2048]{6,5,4,3,2,1,0:T(8,128)(2,1)S(1)}, u32[]{:S(2)}, u32[]{:S(2)}) %collective-permute-start.2) | collective-permute-done | bytes 65568 | tf_op jit(solution)/shard_map/ppermute | solution.py:72
  51.5 6.2 %collective-permute-done.9 = bf16[2,2,1,1,2,8,2048]{6,5,4,3,2,1,0:T(8,128)(2,1)S(1)} collective-permute-done((bf16[2,2,1,1,2,8,2048]{6,5,4,3,2,1,0:T(8,128)(2,1)S(1)}, bf16[2,2,1,1,2,8,2048]{6,5,4,3,2,1,0:T(8,128)(2,1)S(1)}, u32[]{:S(2)}, u32[]{:S(2)}) %collective-permute-start.9) | collective-permute-done | bytes 262176 | tf_op jit(solution)/shard_map/ppermute | solution.py:72
  58.6 6.7 %collective-permute-done.5 = bf16[2,2,2,1,2,8,2048]{6,5,4,3,2,1,0:T(8,128)(2,1)S(1)} collective-permute-done((bf16[2,2,2,1,2,8,2048]{6,5,4,3,2,1,0:T(8,128)(2,1)S(1)}, bf16[2,2,2,1,2,8,2048]{6,5,4,3,2,1,0:T(8,128)(2,1)S(1)}, u32[]{:S(2)}, u32[]{:S(2)}) %collective-permute-start.5) | collective-permute-done | bytes 524320 | tf_op jit(solution)/shard_map/ppermute | solution.py:72
  69.1 3.7 %fusion = f32[256,688]{0,1:T(8,128)S(1)} fusion(bf16[4096,172]{0,1:T(8,128)(2,1)} %collective-permute-done.12, bf16[4096,172]{0,1:T(8,128)(2,1)S(1)} %copy-done.7, bf16[4096,172]{0,1:T(8,128)(2,1)} %collective-permute-done.11, bf16[4096,172]{0,1:T(8,128)(2,1)S(1)} %copy-done.8, f32[4096]{0:T(1024)S(1)} %select_convert_fusion.1, f32[256]{0:T(256)S(1)} %add_rsqrt_fusion, ...), kind=kOutput, calls=%fused_computation | convolution fusion | flops 1472724992 | bytes 8455168 | tf_op jit(solution)/shard_map/dot_general | solution.py:156
  78.2 19.1 %collective-permute-done.14 = f32[2,2,2,1,2,8,2048]{6,5,4,3,2,1,0:T(8,128)S(1)} collective-permute-done((f32[2,2,2,1,2,8,2048]{6,5,4,3,2,1,0:T(8,128)S(1)}, f32[2,2,2,1,2,8,2048]{6,5,4,3,2,1,0:T(8,128)S(1)}, u32[]{:S(2)}, u32[]{:S(2)}) %collective-permute-start.14) | collective-permute-done | bytes 1048608 | tf_op jit(solution)/shard_map/ppermute | solution.py:100
  98.6 3.6 %collective-permute-done.19 = f32[2,2,1,2,2,8,2048]{6,5,4,3,2,1,0:T(8,128)S(1)} collective-permute-done((f32[2,2,1,2,2,8,2048]{6,5,4,3,2,1,0:T(8,128)S(1)}, f32[2,2,1,2,2,8,2048]{6,5,4,3,2,1,0:T(8,128)S(1)}, u32[]{:S(2)}, u32[]{:S(2)}) %collective-permute-start.19) | collective-permute-done | bytes 1048608 | tf_op jit(solution)/shard_map/ppermute | solution.py:100
  102.7 6.9 %collective-permute-done.15 = f32[2,2,1,1,2,8,2048]{6,5,4,3,2,1,0:T(8,128)S(1)} collective-permute-done((f32[2,2,1,1,2,8,2048]{6,5,4,3,2,1,0:T(8,128)S(1)}, f32[2,2,1,1,2,8,2048]{6,5,4,3,2,1,0:T(8,128)S(1)}, u32[]{:S(2)}, u32[]{:S(2)}) %collective-permute-start.15) | collective-permute-done | bytes 524320 | tf_op jit(solution)/shard_map/ppermute | solution.py:100
  116.8 8.3 %collective-permute-done.21 = f32[2,1,1,1,2,8,2048]{6,5,4,3,2,1,0:T(8,128)S(1)} collective-permute-done((f32[2,1,1,1,2,8,2048]{6,5,4,3,2,1,0:T(8,128)S(1)}, f32[2,1,1,1,2,8,2048]{6,5,4,3,2,1,0:T(8,128)S(1)}, u32[]{:S(2)}, u32[]{:S(2)}) %collective-permute-start.21) | collective-permute-done | bytes 262176 | tf_op jit(solution)/shard_map/ppermute | solution.py:100
  147.0 3.4 %collective-permute-done.30 = bf16[1,1,1,1,1,8,2048]{6,5,4,3,2,1,0:T(8,128)(2,1)S(1)} collective-permute-done((bf16[1,1,1,1,1,8,2048]{6,5,4,3,2,1,0:T(8,128)(2,1)S(1)}, bf16[1,1,1,1,1,8,2048]{6,5,4,3,2,1,0:T(8,128)(2,1)S(1)}, u32[]{:S(2)}, u32[]{:S(2)}) %collective-permute-start.30) | collective-permute-done | bytes 32800 | tf_op jit(solution)/shard_map/ppermute | solution.py:72
  151.6 5.9 %collective-permute-done.26 = bf16[2,1,1,1,1,8,2048]{6,5,4,3,2,1,0:T(8,128)(2,1)S(1)} collective-permute-done((bf16[2,1,1,1,1,8,2048]{6,5,4,3,2,1,0:T(8,128)(2,1)S(1)}, bf16[2,1,1,1,1,8,2048]{6,5,4,3,2,1,0:T(8,128)(2,1)S(1)}, u32[]{:S(2)}, u32[]{:S(2)}) %collective-permute-start.26) | collective-permute-done | bytes 65568 | tf_op jit(solution)/shard_map/ppermute | solution.py:72
  159.0 3.7 %collective-permute-done.27 = bf16[2,2,1,1,1,8,2048]{6,5,4,3,2,1,0:T(8,128)(2,1)S(1)} collective-permute-done((bf16[2,2,1,1,1,8,2048]{6,5,4,3,2,1,0:T(8,128)(2,1)S(1)}, bf16[2,2,1,1,1,8,2048]{6,5,4,3,2,1,0:T(8,128)(2,1)S(1)}, u32[]{:S(2)}, u32[]{:S(2)}) %collective-permute-start.27) | collective-permute-done | bytes 131104 | tf_op jit(solution)/shard_map/ppermute | solution.py:72
  167.3 3.4 %collective-permute-done.28 = bf16[2,2,1,1,2,8,2048]{6,5,4,3,2,1,0:T(8,128)(2,1)S(1)} collective-permute-done((bf16[2,2,1,1,2,8,2048]{6,5,4,3,2,1,0:T(8,128)(2,1)S(1)}, bf16[2,2,1,1,2,8,2048]{6,5,4,3,2,1,0:T(8,128)(2,1)S(1)}, u32[]{:S(2)}, u32[]{:S(2)}) %collective-permute-start.28) | collective-permute-done | bytes 262176 | tf_op jit(solution)/shard_map/ppermute | solution.py:72
  170.8 3.3 %collective-permute-start.29 = (bf16[2,2,2,1,2,8,2048]{6,5,4,3,2,1,0:T(8,128)(2,1)S(1)}, bf16[2,2,2,1,2,8,2048]{6,5,4,3,2,1,0:T(8,128)(2,1)S(1)}, u32[]{:S(2)}, u32[]{:S(2)}) collective-permute-start(bf16[2,2,2,1,2,8,2048]{6,5,4,3,2,1,0:T(8,128)(2,1)S(1)} %pad_maximum_fusion.9), channel_id=1, source_target_pairs={{0,6},{2,4},{4,2},{6,0},{8,14},{10,12},{12,10},{14,8},{16,22},{18,... | collective-permute-start | bytes 1572872 | tf_op jit(solution)/shard_map/ppermute | solution.py:72
  174.3 7.0 %collective-permute-done.29 = bf16[2,2,2,1,2,8,2048]{6,5,4,3,2,1,0:T(8,128)(2,1)S(1)} collective-permute-done((bf16[2,2,2,1,2,8,2048]{6,5,4,3,2,1,0:T(8,128)(2,1)S(1)}, bf16[2,2,2,1,2,8,2048]{6,5,4,3,2,1,0:T(8,128)(2,1)S(1)}, u32[]{:S(2)}, u32[]{:S(2)}) %collective-permute-start.29) | collective-permute-done | bytes 524320 | tf_op jit(solution)/shard_map/ppermute | solution.py:72
  186.8 3.9 %broadcast_select_fusion.1 = (bf16[250,4096]{1,0:T(8,128)(2,1)}, bf16[250,4096]{1,0:T(8,128)(2,1)}) fusion(bf16[250,4096]{1,0:T(8,128)(2,1)S(1)} %copy-done.6, bf16[250,4096]{1,0:T(8,128)(2,1)} %param.31, pred[]{:T(512)S(6)} %eq.28), kind=kLoop, calls=%fused_computation.26 | loop fusion | flops 2048000 | bytes 8192001 | tf_op jit(solution)/shard_map/jit(_where)/select_n | solution.py:109
  190.8 4.3 %collective-permute-done.35 = bf16[250,4096]{1,0:T(8,128)(2,1)S(1)} collective-permute-done((bf16[250,4096]{1,0:T(8,128)(2,1)}, bf16[250,4096]{1,0:T(8,128)(2,1)S(1)}, u32[]{:S(2)}, u32[]{:S(2)}) %collective-permute-start.35) | collective-permute-done | bytes 2048032 | tf_op jit(solution)/shard_map/ppermute | solution.py:170
  195.0 74.4 %all-gather.2.cloned.1.call-done = bf16[1024,4096]{1,0:T(8,128)(2,1)} async-done(((bf16[256,4096]{1,0:T(8,128)(2,1)}), bf16[1024,4096]{1,0:T(8,128)(2,1)}) %all-gather.2.cloned.1.call-update) | async-done | bytes 8388624 | tf_op jit(solution)/shard_map/all_gather | solution.py:168
  269.5 7.6 %fusion.49 = (f32[1024]{0:T(1024)S(1)}, f32[1024,500]{0,1:T(8,128)S(1)}) fusion(bf16[1024,4096]{1,0:T(8,128)(2,1)} %all-gather.2.cloned.1.call-done, bf16[250,4096]{1,0:T(8,128)(2,1)S(1)} %collective-permute-done.35, bf16[250,4096]{1,0:T(8,128)(2,1)} %get-tuple-element.63), kind=kOutput, calls=%fused_computation.215 | convolution fusion | flops 4203006976 | bytes 14536704 | tf_op jit(solution)/shard_map/td,vd->tv/dot_general | solution.py:25
  283.6 4.5 %collective-permute-done.38 = f32[2,3,1024]{2,0,1:T(2,128)S(1)} collective-permute-done((f32[2,3,1024]{2,0,1:T(2,128)S(1)}, f32[2,3,1024]{2,0,1:T(2,128)S(1)}, u32[]{:S(2)}, u32[]{:S(2)}) %collective-permute-start.38) | collective-permute-done | bytes 24608 | tf_op jit(solution)/shard_map/ppermute | solution.py:186
  297.3 5.8 %collective-permute-start.41 = (f32[2,3,1024]{2,0,1:T(2,128)S(1)}, f32[2,3,1024]{2,0,1:T(2,128)S(1)}, u32[]{:S(2)}, u32[]{:S(2)}) collective-permute-start(f32[2,3,1024]{2,0,1:T(2,128)S(1)} %pad_maximum_fusion.26), channel_id=1, source_target_pairs={{0,32},{2,34},{4,36},{6,38},{8,40},{10,42},{12,44},{14,46},{16,48}... | collective-permute-start | bytes 73736 | tf_op jit(solution)/shard_map/ppermute | solution.py:186
  (210 shorter events, 104.5 us)
Async XLA Ops:
  7.2 262.3 %all-gather.2.cloned.1.call-start = ((), (), s32[]{:S(2)}) async-start(), calls=%async_computation | async-start | bytes 10485760 | tf_op jit(solution)/shard_map/all_gather | solution.py:168
  8.0 9.3 %collective-permute-start = (bf16[4,4096]{1,0:T(4,128)(2,1)S(1)}, bf16[4,4096]{1,0:T(4,128)(2,1)S(1)}, u32[]{:S(2)}, u32[]{:S(2)}) collective-permute-start(bf16[4,4096]{1,0:T(4,128)(2,1)S(1)} %get-tuple-element.118), channel_id=1, source_target_pairs={{0,1},{1,0},{2,3},{3,2},{4,5},{5,4},{6,7},{7,6},{8,9},{9,8},{10,11... | collective-permute-start | bytes 98312 | tf_op jit(solution)/shard_map/ppermute | solution.py:143
  12.4 55.5 %collective-permute-start.11 = (bf16[4096,172]{0,1:T(8,128)(2,1)}, bf16[4096,172]{0,1:T(8,128)(2,1)}, u32[]{:S(2)}, u32[]{:S(2)}) collective-permute-start(bf16[4096,172]{0,1:T(8,128)(2,1)} %get-tuple-element.45), channel_id=1, source_target_pairs={{0,1},{1,0},{2,3},{3,2},{4,5},{5,4},{6,7},{7,6},{8,9},{9,8},{10,11... | collective-permute-start | bytes 4227080 | tf_op jit(solution)/shard_map/ppermute | solution.py:141
  12.9 55.0 %collective-permute-start.12 = (bf16[4096,172]{0,1:T(8,128)(2,1)}, bf16[4096,172]{0,1:T(8,128)(2,1)}, u32[]{:S(2)}, u32[]{:S(2)}) collective-permute-start(bf16[4096,172]{0,1:T(8,128)(2,1)} %get-tuple-element.46), channel_id=1, source_target_pairs={{0,1},{1,0},{2,3},{3,2},{4,5},{5,4},{6,7},{7,6},{8,9},{9,8},{10,11... | collective-permute-start | bytes 4227080 | tf_op jit(solution)/shard_map/ppermute | solution.py:141
  12.9 59.8 %collective-permute-start.13 = (bf16[172,4096]{1,0:T(8,128)(2,1)S(1)}, bf16[172,4096]{1,0:T(8,128)(2,1)}, u32[]{:S(2)}, u32[]{:S(2)}) collective-permute-start(bf16[172,4096]{1,0:T(8,128)(2,1)S(1)} %get-tuple-element.20), channel_id=1, source_target_pairs={{0,1},{1,0},{2,3},{3,2},{4,5},{5,4},{6,7},{7,6},{8,9},{9,8},{10,11... | collective-permute-start | bytes 4227080 | tf_op jit(solution)/shard_map/ppermute | solution.py:141
  17.4 9.2 %collective-permute-start.1 = (bf16[1,1,1,1,1,8,2048]{6,5,4,3,2,1,0:T(8,128)(2,1)S(1)}, bf16[1,1,1,1,1,8,2048]{6,5,4,3,2,1,0:T(8,128)(2,1)S(1)}, u32[]{:S(2)}, u32[]{:S(2)}) collective-permute-start(bf16[1,1,1,1,1,8,2048]{6,5,4,3,2,1,0:T(8,128)(2,1)S(1)} %get-tuple-element.115), channel_id=1, source_target_pairs={{0,32},{2,34},{4,36},{6,38},{8,40},{10,42},{12,44},{14,46},{16,48}... | collective-permute-start | bytes 98312 | tf_op jit(solution)/shard_map/ppermute | solution.py:72
  24.7 8.2 %collective-permute-start.6 = (bf16[1,1,1,1,1,8,2048]{6,5,4,3,2,1,0:T(8,128)(2,1)S(1)}, bf16[1,1,1,1,1,8,2048]{6,5,4,3,2,1,0:T(8,128)(2,1)S(1)}, u32[]{:S(2)}, u32[]{:S(2)}) collective-permute-start(bf16[1,1,1,1,1,8,2048]{6,5,4,3,2,1,0:T(8,128)(2,1)S(1)} %get-tuple-element.116), channel_id=1, source_target_pairs={{0,32},{2,34},{4,36},{6,38},{8,40},{10,42},{12,44},{14,46},{16,48}... | collective-permute-start | bytes 98312 | tf_op jit(solution)/shard_map/ppermute | solution.py:72
  47.2 10.4 %collective-permute-start.9 = (bf16[2,2,1,1,2,8,2048]{6,5,4,3,2,1,0:T(8,128)(2,1)S(1)}, bf16[2,2,1,1,2,8,2048]{6,5,4,3,2,1,0:T(8,128)(2,1)S(1)}, u32[]{:S(2)}, u32[]{:S(2)}) collective-permute-start(bf16[2,2,1,1,2,8,2048]{6,5,4,3,2,1,0:T(8,128)(2,1)S(1)} %pad_maximum_fusion.12), channel_id=1, source_target_pairs={{0,6},{2,4},{4,2},{6,0},{8,14},{10,12},{12,10},{14,8},{16,22},{18,... | collective-permute-start | bytes 786440 | tf_op jit(solution)/shard_map/ppermute | solution.py:72
  50.6 14.8 %collective-permute-start.5 = (bf16[2,2,2,1,2,8,2048]{6,5,4,3,2,1,0:T(8,128)(2,1)S(1)}, bf16[2,2,2,1,2,8,2048]{6,5,4,3,2,1,0:T(8,128)(2,1)S(1)}, u32[]{:S(2)}, u32[]{:S(2)}) collective-permute-start(bf16[2,2,2,1,2,8,2048]{6,5,4,3,2,1,0:T(8,128)(2,1)S(1)} %pad_maximum_fusion.7), channel_id=1, source_target_pairs={{0,6},{2,4},{4,2},{6,0},{8,14},{10,12},{12,10},{14,8},{16,22},{18,... | collective-permute-start | bytes 1572872 | tf_op jit(solution)/shard_map/ppermute | solution.py:72
  57.7 9.4 %collective-permute-start.10 = (bf16[2,2,1,2,2,8,2048]{6,5,4,3,2,1,0:T(8,128)(2,1)S(1)}, bf16[2,2,1,2,2,8,2048]{6,5,4,3,2,1,0:T(8,128)(2,1)S(1)}, u32[]{:S(2)}, u32[]{:S(2)}) collective-permute-start(bf16[2,2,1,2,2,8,2048]{6,5,4,3,2,1,0:T(8,128)(2,1)S(1)} %pad_maximum_fusion.8), channel_id=1, source_target_pairs={{0,8},{2,10},{4,12},{6,14},{8,0},{10,2},{12,4},{14,6},{16,24},{18,... | collective-permute-start | bytes 1572872 | tf_op jit(solution)/shard_map/ppermute | solution.py:72
  76.1 21.2 %collective-permute-start.14 = (f32[2,2,2,1,2,8,2048]{6,5,4,3,2,1,0:T(8,128)S(1)}, f32[2,2,2,1,2,8,2048]{6,5,4,3,2,1,0:T(8,128)S(1)}, u32[]{:S(2)}, u32[]{:S(2)}) collective-permute-start(f32[2,2,2,1,2,8,2048]{6,5,4,3,2,1,0:T(8,128)S(1)} %slice_select_fusion.1), channel_id=1, source_target_pairs={{0,6},{2,4},{4,2},{6,0},{8,14},{10,12},{12,10},{14,8},{16,22},{18,... | collective-permute-start | bytes 3145736 | tf_op jit(solution)/shard_map/ppermute | solution.py:100
  77.4 24.9 %collective-permute-start.19 = (f32[2,2,1,2,2,8,2048]{6,5,4,3,2,1,0:T(8,128)S(1)}, f32[2,2,1,2,2,8,2048]{6,5,4,3,2,1,0:T(8,128)S(1)}, u32[]{:S(2)}, u32[]{:S(2)}) collective-permute-start(f32[2,2,1,2,2,8,2048]{6,5,4,3,2,1,0:T(8,128)S(1)} %slice_select_fusion), channel_id=1, source_target_pairs={{0,8},{2,10},{4,12},{6,14},{8,0},{10,2},{12,4},{14,6},{16,24},{18,... | collective-permute-start | bytes 3145736 | tf_op jit(solution)/shard_map/ppermute | solution.py:100
  97.6 11.9 %collective-permute-start.15 = (f32[2,2,1,1,2,8,2048]{6,5,4,3,2,1,0:T(8,128)S(1)}, f32[2,2,1,1,2,8,2048]{6,5,4,3,2,1,0:T(8,128)S(1)}, u32[]{:S(2)}, u32[]{:S(2)}) collective-permute-start(f32[2,2,1,1,2,8,2048]{6,5,4,3,2,1,0:T(8,128)S(1)} %slice_select_fusion.3), channel_id=1, source_target_pairs={{0,8},{2,10},{4,12},{6,14},{8,0},{10,2},{12,4},{14,6},{16,24},{18,... | collective-permute-start | bytes 1572872 | tf_op jit(solution)/shard_map/ppermute | solution.py:100
  102.6 10.5 %collective-permute-start.20 = (f32[2,2,1,1,2,8,2048]{6,5,4,3,2,1,0:T(8,128)S(1)}, f32[2,2,1,1,2,8,2048]{6,5,4,3,2,1,0:T(8,128)S(1)}, u32[]{:S(2)}, u32[]{:S(2)}) collective-permute-start(f32[2,2,1,1,2,8,2048]{6,5,4,3,2,1,0:T(8,128)S(1)} %slice_select_fusion.2), channel_id=1, source_target_pairs={{0,6},{2,4},{4,2},{6,0},{8,14},{10,12},{12,10},{14,8},{16,22},{18,... | collective-permute-start | bytes 1572872 | tf_op jit(solution)/shard_map/ppermute | solution.py:100
  113.2 11.9 %collective-permute-start.21 = (f32[2,1,1,1,2,8,2048]{6,5,4,3,2,1,0:T(8,128)S(1)}, f32[2,1,1,1,2,8,2048]{6,5,4,3,2,1,0:T(8,128)S(1)}, u32[]{:S(2)}, u32[]{:S(2)}) collective-permute-start(f32[2,1,1,1,2,8,2048]{6,5,4,3,2,1,0:T(8,128)S(1)} %slice_select_fusion.4), channel_id=1, source_target_pairs={{0,16},{2,18},{4,20},{6,22},{8,24},{10,26},{12,28},{14,30},{16,0},... | collective-permute-start | bytes 786440 | tf_op jit(solution)/shard_map/ppermute | solution.py:100
  116.2 10.4 %collective-permute-start.17 = (f32[2,1,1,1,1,8,2048]{6,5,4,3,2,1,0:T(8,128)S(1)}, f32[2,1,1,1,1,8,2048]{6,5,4,3,2,1,0:T(8,128)S(1)}, u32[]{:S(2)}, u32[]{:S(2)}) collective-permute-start(f32[2,1,1,1,1,8,2048]{6,5,4,3,2,1,0:T(8,128)S(1)} %slice_select_fusion.7), channel_id=1, source_target_pairs={{0,16},{2,18},{4,20},{6,22},{8,24},{10,26},{12,28},{14,30},{16,0},... | collective-permute-start | bytes 393224 | tf_op jit(solution)/shard_map/ppermute | solution.py:100
  126.7 8.7 %collective-permute-start.18 = (f32[1,1,1,1,1,8,2048]{6,5,4,3,2,1,0:T(8,128)S(1)}, f32[1,1,1,1,1,8,2048]{6,5,4,3,2,1,0:T(8,128)S(1)}, u32[]{:S(2)}, u32[]{:S(2)}) collective-permute-start(f32[1,1,1,1,1,8,2048]{6,5,4,3,2,1,0:T(8,128)S(1)} %slice_select_fusion.9), channel_id=1, source_target_pairs={{0,32},{2,34},{4,36},{6,38},{8,40},{10,42},{12,44},{14,46},{16,48}... | collective-permute-start | bytes 196616 | tf_op jit(solution)/shard_map/ppermute | solution.py:100
  130.2 8.5 %collective-permute-start.23 = (f32[1,1,1,1,1,8,2048]{6,5,4,3,2,1,0:T(8,128)S(1)}, f32[1,1,1,1,1,8,2048]{6,5,4,3,2,1,0:T(8,128)S(1)}, u32[]{:S(2)}, u32[]{:S(2)}) collective-permute-start(f32[1,1,1,1,1,8,2048]{6,5,4,3,2,1,0:T(8,128)S(1)} %slice_select_fusion.8), channel_id=1, source_target_pairs={{0,32},{2,34},{4,36},{6,38},{8,40},{10,42},{12,44},{14,46},{16,48}... | collective-permute-start | bytes 196616 | tf_op jit(solution)/shard_map/ppermute | solution.py:100
  139.0 8.0 %collective-permute-start.25 = (bf16[1,1,1,1,1,8,2048]{6,5,4,3,2,1,0:T(8,128)(2,1)S(1)}, bf16[1,1,1,1,1,8,2048]{6,5,4,3,2,1,0:T(8,128)(2,1)S(1)}, u32[]{:S(2)}, u32[]{:S(2)}) collective-permute-start(bf16[1,1,1,1,1,8,2048]{6,5,4,3,2,1,0:T(8,128)(2,1)S(1)} %get-tuple-element.111), channel_id=1, source_target_pairs={{0,32},{2,34},{4,36},{6,38},{8,40},{10,42},{12,44},{14,46},{16,48}... | collective-permute-start | bytes 98312 | tf_op jit(solution)/shard_map/ppermute | solution.py:72
  142.2 8.2 %collective-permute-start.30 = (bf16[1,1,1,1,1,8,2048]{6,5,4,3,2,1,0:T(8,128)(2,1)S(1)}, bf16[1,1,1,1,1,8,2048]{6,5,4,3,2,1,0:T(8,128)(2,1)S(1)}, u32[]{:S(2)}, u32[]{:S(2)}) collective-permute-start(bf16[1,1,1,1,1,8,2048]{6,5,4,3,2,1,0:T(8,128)(2,1)S(1)} %get-tuple-element.112), channel_id=1, source_target_pairs={{0,32},{2,34},{4,36},{6,38},{8,40},{10,42},{12,44},{14,46},{16,48}... | collective-permute-start | bytes 98312 | tf_op jit(solution)/shard_map/ppermute | solution.py:72
  150.5 8.3 %collective-permute-start.31 = (bf16[2,1,1,1,1,8,2048]{6,5,4,3,2,1,0:T(8,128)(2,1)S(1)}, bf16[2,1,1,1,1,8,2048]{6,5,4,3,2,1,0:T(8,128)(2,1)S(1)}, u32[]{:S(2)}, u32[]{:S(2)}) collective-permute-start(bf16[2,1,1,1,1,8,2048]{6,5,4,3,2,1,0:T(8,128)(2,1)S(1)} %pad_maximum_fusion.22), channel_id=1, source_target_pairs={{0,2},{2,0},{4,6},{6,4},{8,10},{10,8},{12,14},{14,12},{16,18},{18,... | collective-permute-start | bytes 196616 | tf_op jit(solution)/shard_map/ppermute | solution.py:72
  165.1 9.0 %collective-permute-start.33 = (bf16[2,2,1,1,2,8,2048]{6,5,4,3,2,1,0:T(8,128)(2,1)S(1)}, bf16[2,2,1,1,2,8,2048]{6,5,4,3,2,1,0:T(8,128)(2,1)S(1)}, u32[]{:S(2)}, u32[]{:S(2)}) collective-permute-start(bf16[2,2,1,1,2,8,2048]{6,5,4,3,2,1,0:T(8,128)(2,1)S(1)} %pad_maximum_fusion.14), channel_id=1, source_target_pairs={{0,6},{2,4},{4,2},{6,0},{8,14},{10,12},{12,10},{14,8},{16,22},{18,... | collective-permute-start | bytes 786440 | tf_op jit(solution)/shard_map/ppermute | solution.py:72
  170.8 10.5 %collective-permute-start.29 = (bf16[2,2,2,1,2,8,2048]{6,5,4,3,2,1,0:T(8,128)(2,1)S(1)}, bf16[2,2,2,1,2,8,2048]{6,5,4,3,2,1,0:T(8,128)(2,1)S(1)}, u32[]{:S(2)}, u32[]{:S(2)}) collective-permute-start(bf16[2,2,2,1,2,8,2048]{6,5,4,3,2,1,0:T(8,128)(2,1)S(1)} %pad_maximum_fusion.9), channel_id=1, source_target_pairs={{0,6},{2,4},{4,2},{6,0},{8,14},{10,12},{12,10},{14,8},{16,22},{18,... | collective-permute-start | bytes 1572872 | tf_op jit(solution)/shard_map/ppermute | solution.py:72
  174.2 9.3 %collective-permute-start.34 = (bf16[2,2,1,2,2,8,2048]{6,5,4,3,2,1,0:T(8,128)(2,1)S(1)}, bf16[2,2,1,2,2,8,2048]{6,5,4,3,2,1,0:T(8,128)(2,1)S(1)}, u32[]{:S(2)}, u32[]{:S(2)}) collective-permute-start(bf16[2,2,1,2,2,8,2048]{6,5,4,3,2,1,0:T(8,128)(2,1)S(1)} %pad_maximum_fusion.10), channel_id=1, source_target_pairs={{0,8},{2,10},{4,12},{6,14},{8,0},{10,2},{12,4},{14,6},{16,24},{18,... | collective-permute-start | bytes 1572872 | tf_op jit(solution)/shard_map/ppermute | solution.py:72
  (34 other events, 195.0 us)
Sparse Core Ops, SparseCore 0:
  185.3 84.0 all-gather.1
where the time goes:
time: 322 us
  waiting for transfers between devices  214 us (66%)
  starting transfers between devices  55.5 us (17%)
  other arithmetic  16.5 us (5%)
  between operations  14.8 us (5%)
  matrix products  14 us (4%)
  local copies, waits for them, and re-layouts  7.67 us (2%)
    all_gather x1, waiting for transfers between devices, per_device(): every = lax.all_gather(final, 'grp', axis=0, tiled=True)  74.4 us
    ppermute x20, waiting for transfers between devices, gather_doubling(): lax.ppermute(held, 'zx', [(i, i ^ partner_mask(bit)) for i in range(size)])  62.5 us
    ppermute x10, waiting for transfers between devices, scatter_halving(): lax.ppermute(jnp.where(low, upper, lower), 'zx', [(i, i ^ partner_mask(bi...  52.9 us
    ppermute x20, starting transfers between devices, gather_doubling(): lax.ppermute(held, 'zx', [(i, i ^ partner_mask(bit)) for i in range(size)])  30.3 us
    ppermute x7, waiting for transfers between devices, per_device(): lax.ppermute(state, axis, [(i, i ^ partner_mask(bit)) for i in range(size)])  18.3 us
    ppermute x7, starting transfers between devices, per_device(): lax.ppermute(state, axis, [(i, i ^ partner_mask(bit)) for i in range(size)])  15.5 us
    ppermute x10, starting transfers between devices, scatter_halving(): lax.ppermute(jnp.where(low, upper, lower), 'zx', [(i, i ^ partner_mask(bi...  8.42 us
    dot_general x1, matrix products, vocab_terms(): jnp.einsum('td,vd->tv', token_rows, head_rows, preferred_element_type=jnp...  7.62 us
  transfers between devices with their start and end apart: 45, of which 36 were waited for; matrix products, arithmetic and copies ran while one was open for 6% of the time, Pallas kernels for 0%

commit v1 on v0

--- a/solution.py
+++ b/solution.py
@@ -138,7 +138,9 @@
 
     pol_w = (pol_gate, pol_up, pol_down)
     ref_w = (ref_gate, ref_up, ref_down)
-    got_w = lax.ppermute(lax.cond(first, lambda: ref_w, lambda: pol_w), "core", SWAP)
+    got_pol = lax.ppermute(pol_w, "core", [(1, 0)])
+    got_ref = lax.ppermute(ref_w, "core", [(0, 1)])
+    got_w = [jnp.where(first, p, r) for p, r in zip(got_pol, got_ref)]
     keep_h, give_h = pick(first, pol_hidden, ref_hidden)
     got_h = lax.ppermute(give_h, "core", SWAP)
     pair_rows = jnp.where(
@@ -166,8 +168,12 @@
     ref_out = jnp.where(first, sent_out, mine_out)
 
     every = lax.all_gather(final, "grp", axis=0, tiled=True)
-    keep_v, give_v = pick(first, pol_head, ref_head)
-    got_v = lax.ppermute(give_v, "core", SWAP)
+    keep_v = jnp.where(first, pol_head, ref_head)
+    got_v = jnp.where(
+        first,
+        lax.ppermute(pol_head, "core", [(1, 0)]),
+        lax.ppermute(ref_head, "core", [(0, 1)]),
+    )
     voc_dev = pol_head.shape[0]
     positions = jnp.arange(every.shape[0], dtype=jnp.int32)
     base = group * per_group

time: 322 us -> 356 us (1.11)
  waiting for transfers between devices: 214 us -> 232 us
  starting transfers between devices: 55.5 us -> 72.1 us
  other arithmetic: 16.5 us -> 22 us
  local copies, waits for them, and re-layouts: 7.67 us -> 3.91 us
    ppermute x20, waiting for transfers between devices: 62.5 us -> 86.8 us  [gather_doubling(): lax.ppermute(held, 'zx', [(i, i ^ partner_mask(bit)) for i in range(size)])]
    ppermute x4 -> x8, starting transfers between devices: 0.95 us -> 21 us  [the longest x3 10.1 us: per_device(): got_ref = lax.ppermute(ref_w, 'core', [(0, 1)])]
    select_n x0 -> x5, other arithmetic: none -> 8.52 us  [the longest x1 3.61 us: per_device(): jnp.where(first, lax.ppermute(pol_head, 'core', [(1, 0)]), lax.ppermute(r...]
    ppermute x20, starting transfers between devices: 30.3 us -> 23.6 us  [gather_doubling(): lax.ppermute(held, 'zx', [(i, i ^ partner_mask(bit)) for i in range(size)])]
    all_gather x1, waiting for transfers between devices: 74.4 us -> 69.3 us  [per_device(): every = lax.all_gather(final, 'grp', axis=0, tiled=True)]
    cond x7 -> x0, local copies, waits for them, and re-layouts: 4.27 us -> none
    select_n x2 -> x1, other arithmetic: 4.71 us -> 0.81 us  [pick(): return (jnp.where(first, pol, ref), jnp.where(first, ref, pol))]
    ppermute x10, starting transfers between devices: 8.42 us -> 12.2 us  [scatter_halving(): lax.ppermute(jnp.where(low, upper, lower), 'zx', [(i, i ^ partner_mask(bi...]
  transfers between devices with their start and end apart: 45 -> 49, of which waited for: 36 -> 37; matrix products, arithmetic and copies ran while one was open for 6% -> 5% of each run, Pallas kernels for 0% -> 0%
where the time goes in v1:
time: 356 us
  waiting for transfers between devices  232 us (65%)
  starting transfers between devices  72.1 us (20%)
  other arithmetic  22 us (6%)
  between operations  14.9 us (4%)
  matrix products  10.8 us (3%)
  local copies, waits for them, and re-layouts  3.91 us (1%)
    ppermute x20, waiting for transfers between devices, gather_doubling(): lax.ppermute(held, 'zx', [(i, i ^ partner_mask(bit)) for i in range(size)])  86.8 us
    all_gather x1, waiting for transfers between devices, per_device(): every = lax.all_gather(final, 'grp', axis=0, tiled=True)  69.3 us
    ppermute x10, waiting for transfers between devices, scatter_halving(): lax.ppermute(jnp.where(low, upper, lower), 'zx', [(i, i ^ partner_mask(bi...  55.2 us
    ppermute x20, starting transfers between devices, gather_doubling(): lax.ppermute(held, 'zx', [(i, i ^ partner_mask(bit)) for i in range(size)])  23.6 us
    ppermute x7, waiting for transfers between devices, per_device(): lax.ppermute(state, axis, [(i, i ^ partner_mask(bit)) for i in range(size)])  18.5 us
    ppermute x7, starting transfers between devices, per_device(): lax.ppermute(state, axis, [(i, i ^ partner_mask(bit)) for i in range(size)])  15 us
    ppermute x10, starting transfers between devices, scatter_halving(): lax.ppermute(jnp.where(low, upper, lower), 'zx', [(i, i ^ partner_mask(bi...  12.2 us
    ppermute x3, starting transfers between devices, per_device(): got_ref = lax.ppermute(ref_w, 'core', [(0, 1)])  10.1 us
  transfers between devices with their start and end apart: 49, of which 37 were waited for; matrix products, arithmetic and copies ran while one was open for 5% of the time, Pallas kernels for 0%

profile of v1, /device:TPU:6, one launch (start us, length us, event | category | flops | bytes accessed | tf_op | source)
XLA Modules:
  0.0 355.9 jit_solution(2873529470405291476)
XLA Ops:
  9.6 5.2 %collective-permute-start.14 = (bf16[4096,172]{0,1:T(8,128)(2,1)}, bf16[4096,172]{0,1:T(8,128)(2,1)}, u32[]{:S(2)}, u32[]{:S(2)}) collective-permute-start(bf16[4096,172]{0,1:T(8,128)(2,1)} %param.26), channel_id=1, source_target_pairs={{0,1},{2,3},{4,5},{6,7},{8,9},{10,11},{12,13},{14,15},{16,17},{18,... | collective-permute-start | bytes 4227080 | tf_op jit(solution)/shard_map/ppermute | solution.py:142
  16.1 3.7 %broadcast_select_fusion.5 = (bf16[4096,172]{0,1:T(8,128)(2,1)}, bf16[4096,172]{0,1:T(8,128)(2,1)}) fusion(bf16[4096,172]{0,1:T(8,128)(2,1)} %param.23, bf16[4096,172]{0,1:T(8,128)(2,1)} %param.26, pred[]{:T(512)S(6)} %eq.28, bf16[4096,172]{0,1:T(8,128)(2,1)} %param.22, bf16[4096,172]{0,1:T(8,128)(2,1)} %param.25), kind=kLoop, calls=%fused_computation.32 | loop fusion | flops 1409024 | bytes 8454145 | tf_op jit(solution)/shard_map/jit(_where)/select_n | solution.py:153
  19.9 7.3 %collective-permute-start.1 = (bf16[1,1,1,1,1,8,2048]{6,5,4,3,2,1,0:T(8,128)(2,1)S(1)}, bf16[1,1,1,1,1,8,2048]{6,5,4,3,2,1,0:T(8,128)(2,1)S(1)}, u32[]{:S(2)}, u32[]{:S(2)}) collective-permute-start(bf16[1,1,1,1,1,8,2048]{6,5,4,3,2,1,0:T(8,128)(2,1)S(1)} %get-tuple-element.69), channel_id=1, source_target_pairs={{0,32},{2,34},{4,36},{6,38},{8,40},{10,42},{12,44},{14,46},{16,48}... | collective-permute-start | bytes 98312 | tf_op jit(solution)/shard_map/ppermute | solution.py:72
  29.0 6.5 %collective-permute-done.6 = bf16[1,1,1,1,1,8,2048]{6,5,4,3,2,1,0:T(8,128)(2,1)S(1)} collective-permute-done((bf16[1,1,1,1,1,8,2048]{6,5,4,3,2,1,0:T(8,128)(2,1)S(1)}, bf16[1,1,1,1,1,8,2048]{6,5,4,3,2,1,0:T(8,128)(2,1)S(1)}, u32[]{:S(2)}, u32[]{:S(2)}) %collective-permute-start.6) | collective-permute-done | bytes 32800 | tf_op jit(solution)/shard_map/ppermute | solution.py:72
  37.5 4.7 %collective-permute-done.2 = bf16[2,1,1,1,1,8,2048]{6,5,4,3,2,1,0:T(8,128)(2,1)S(1)} collective-permute-done((bf16[2,1,1,1,1,8,2048]{6,5,4,3,2,1,0:T(8,128)(2,1)S(1)}, bf16[2,1,1,1,1,8,2048]{6,5,4,3,2,1,0:T(8,128)(2,1)S(1)}, u32[]{:S(2)}, u32[]{:S(2)}) %collective-permute-start.2) | collective-permute-done | bytes 65568 | tf_op jit(solution)/shard_map/ppermute | solution.py:72
  44.8 4.1 %collective-permute-done.3 = bf16[2,2,1,1,1,8,2048]{6,5,4,3,2,1,0:T(8,128)(2,1)S(1)} collective-permute-done((bf16[2,2,1,1,1,8,2048]{6,5,4,3,2,1,0:T(8,128)(2,1)S(1)}, bf16[2,2,1,1,1,8,2048]{6,5,4,3,2,1,0:T(8,128)(2,1)S(1)}, u32[]{:S(2)}, u32[]{:S(2)}) %collective-permute-start.3) | collective-permute-done | bytes 131104 | tf_op jit(solution)/shard_map/ppermute | solution.py:72
  49.7 6.3 %collective-permute-done.8 = bf16[2,1,1,1,2,8,2048]{6,5,4,3,2,1,0:T(8,128)(2,1)S(1)} collective-permute-done((bf16[2,1,1,1,2,8,2048]{6,5,4,3,2,1,0:T(8,128)(2,1)S(1)}, bf16[2,1,1,1,2,8,2048]{6,5,4,3,2,1,0:T(8,128)(2,1)S(1)}, u32[]{:S(2)}, u32[]{:S(2)}) %collective-permute-start.8) | collective-permute-done | bytes 131104 | tf_op jit(solution)/shard_map/ppermute | solution.py:72
  56.0 6.3 %collective-permute-done.4 = bf16[2,2,1,1,2,8,2048]{6,5,4,3,2,1,0:T(8,128)(2,1)S(1)} collective-permute-done((bf16[2,2,1,1,2,8,2048]{6,5,4,3,2,1,0:T(8,128)(2,1)S(1)}, bf16[2,2,1,1,2,8,2048]{6,5,4,3,2,1,0:T(8,128)(2,1)S(1)}, u32[]{:S(2)}, u32[]{:S(2)}) %collective-permute-start.4) | collective-permute-done | bytes 262176 | tf_op jit(solution)/shard_map/ppermute | solution.py:72
  62.9 8.1 %collective-permute-done.9 = bf16[2,2,1,1,2,8,2048]{6,5,4,3,2,1,0:T(8,128)(2,1)S(1)} collective-permute-done((bf16[2,2,1,1,2,8,2048]{6,5,4,3,2,1,0:T(8,128)(2,1)S(1)}, bf16[2,2,1,1,2,8,2048]{6,5,4,3,2,1,0:T(8,128)(2,1)S(1)}, u32[]{:S(2)}, u32[]{:S(2)}) %collective-permute-start.9) | collective-permute-done | bytes 262176 | tf_op jit(solution)/shard_map/ppermute | solution.py:72
  71.6 9.8 %collective-permute-done.5 = bf16[2,2,2,1,2,8,2048]{6,5,4,3,2,1,0:T(8,128)(2,1)S(1)} collective-permute-done((bf16[2,2,2,1,2,8,2048]{6,5,4,3,2,1,0:T(8,128)(2,1)S(1)}, bf16[2,2,2,1,2,8,2048]{6,5,4,3,2,1,0:T(8,128)(2,1)S(1)}, u32[]{:S(2)}, u32[]{:S(2)}) %collective-permute-start.5) | collective-permute-done | bytes 524320 | tf_op jit(solution)/shard_map/ppermute | solution.py:72
  81.7 8.9 %collective-permute-done.10 = bf16[2,2,1,2,2,8,2048]{6,5,4,3,2,1,0:T(8,128)(2,1)S(1)} collective-permute-done((bf16[2,2,1,2,2,8,2048]{6,5,4,3,2,1,0:T(8,128)(2,1)S(1)}, bf16[2,2,1,2,2,8,2048]{6,5,4,3,2,1,0:T(8,128)(2,1)S(1)}, u32[]{:S(2)}, u32[]{:S(2)}) %collective-permute-start.10) | collective-permute-done | bytes 524320 | tf_op jit(solution)/shard_map/ppermute | solution.py:72
  105.9 24.3 %collective-permute-done.17 = f32[2,2,2,1,2,8,2048]{6,5,4,3,2,1,0:T(8,128)S(1)} collective-permute-done((f32[2,2,2,1,2,8,2048]{6,5,4,3,2,1,0:T(8,128)S(1)}, f32[2,2,2,1,2,8,2048]{6,5,4,3,2,1,0:T(8,128)S(1)}, u32[]{:S(2)}, u32[]{:S(2)}) %collective-permute-start.17) | collective-permute-done | bytes 1048608 | tf_op jit(solution)/shard_map/ppermute | solution.py:100
  133.0 9.3 %collective-permute-done.18 = f32[2,2,1,1,2,8,2048]{6,5,4,3,2,1,0:T(8,128)S(1)} collective-permute-done((f32[2,2,1,1,2,8,2048]{6,5,4,3,2,1,0:T(8,128)S(1)}, f32[2,2,1,1,2,8,2048]{6,5,4,3,2,1,0:T(8,128)S(1)}, u32[]{:S(2)}, u32[]{:S(2)}) %collective-permute-start.18) | collective-permute-done | bytes 524320 | tf_op jit(solution)/shard_map/ppermute | solution.py:100
  149.8 10.1 %collective-permute-done.24 = f32[2,1,1,1,2,8,2048]{6,5,4,3,2,1,0:T(8,128)S(1)} collective-permute-done((f32[2,1,1,1,2,8,2048]{6,5,4,3,2,1,0:T(8,128)S(1)}, f32[2,1,1,1,2,8,2048]{6,5,4,3,2,1,0:T(8,128)S(1)}, u32[]{:S(2)}, u32[]{:S(2)}) %collective-permute-start.24) | collective-permute-done | bytes 262176 | tf_op jit(solution)/shard_map/ppermute | solution.py:100
  185.9 6.0 %collective-permute-done.29 = bf16[2,1,1,1,1,8,2048]{6,5,4,3,2,1,0:T(8,128)(2,1)S(1)} collective-permute-done((bf16[2,1,1,1,1,8,2048]{6,5,4,3,2,1,0:T(8,128)(2,1)S(1)}, bf16[2,1,1,1,1,8,2048]{6,5,4,3,2,1,0:T(8,128)(2,1)S(1)}, u32[]{:S(2)}, u32[]{:S(2)}) %collective-permute-start.29) | collective-permute-done | bytes 65568 | tf_op jit(solution)/shard_map/ppermute | solution.py:72
  193.0 4.1 %collective-permute-done.30 = bf16[2,2,1,1,1,8,2048]{6,5,4,3,2,1,0:T(8,128)(2,1)S(1)} collective-permute-done((bf16[2,2,1,1,1,8,2048]{6,5,4,3,2,1,0:T(8,128)(2,1)S(1)}, bf16[2,2,1,1,1,8,2048]{6,5,4,3,2,1,0:T(8,128)(2,1)S(1)}, u32[]{:S(2)}, u32[]{:S(2)}) %collective-permute-start.30) | collective-permute-done | bytes 131104 | tf_op jit(solution)/shard_map/ppermute | solution.py:72
  201.5 3.7 %collective-permute-done.31 = bf16[2,2,1,1,2,8,2048]{6,5,4,3,2,1,0:T(8,128)(2,1)S(1)} collective-permute-done((bf16[2,2,1,1,2,8,2048]{6,5,4,3,2,1,0:T(8,128)(2,1)S(1)}, bf16[2,2,1,1,2,8,2048]{6,5,4,3,2,1,0:T(8,128)(2,1)S(1)}, u32[]{:S(2)}, u32[]{:S(2)}) %collective-permute-start.31) | collective-permute-done | bytes 262176 | tf_op jit(solution)/shard_map/ppermute | solution.py:72
  208.8 6.9 %collective-permute-done.32 = bf16[2,2,2,1,2,8,2048]{6,5,4,3,2,1,0:T(8,128)(2,1)S(1)} collective-permute-done((bf16[2,2,2,1,2,8,2048]{6,5,4,3,2,1,0:T(8,128)(2,1)S(1)}, bf16[2,2,2,1,2,8,2048]{6,5,4,3,2,1,0:T(8,128)(2,1)S(1)}, u32[]{:S(2)}, u32[]{:S(2)}) %collective-permute-start.32) | collective-permute-done | bytes 524320 | tf_op jit(solution)/shard_map/ppermute | solution.py:72
  222.3 5.6 %collective-permute-start.39 = (bf16[250,4096]{1,0:T(8,128)(2,1)}, bf16[250,4096]{1,0:T(8,128)(2,1)}, u32[]{:S(2)}, u32[]{:S(2)}) collective-permute-start(bf16[250,4096]{1,0:T(8,128)(2,1)} %param.29), channel_id=1, source_target_pairs={{0,1},{2,3},{4,5},{6,7},{8,9},{10,11},{12,13},{14,15},{16,17},{18,... | collective-permute-start | bytes 6144008 | tf_op jit(solution)/shard_map/ppermute | solution.py:175
  230.8 3.6 %broadcast_select_fusion = bf16[250,4096]{1,0:T(8,128)(2,1)} fusion(bf16[250,4096]{1,0:T(8,128)(2,1)} %collective-permute-done.38, bf16[250,4096]{1,0:T(8,128)(2,1)} %collective-permute-done.39, pred[]{:T(512)S(6)} %eq.28), kind=kLoop, calls=%fused_computation.25 | loop fusion | flops 1024000 | bytes 6144001 | tf_op jit(solution)/shard_map/jit(_where)/select_n | solution.py:172
  234.4 69.3 %all-gather.2.cloned.1.call-done = bf16[1024,4096]{1,0:T(8,128)(2,1)} async-done(((bf16[256,4096]{1,0:T(8,128)(2,1)}), bf16[1024,4096]{1,0:T(8,128)(2,1)}) %all-gather.2.cloned.1.call-update) | async-done | bytes 8388624 | tf_op jit(solution)/shard_map/all_gather | solution.py:170
  303.7 7.6 %fusion.49 = (f32[1024]{0:T(1024)S(1)}, f32[1024,500]{0,1:T(8,128)S(1)}) fusion(bf16[1024,4096]{1,0:T(8,128)(2,1)} %all-gather.2.cloned.1.call-done, bf16[250,4096]{1,0:T(8,128)(2,1)} %broadcast_select_fusion, bf16[250,4096]{1,0:T(8,128)(2,1)S(1)} %copy-done.1), kind=kOutput, calls=%fused_computation.218 | convolution fusion | flops 4203006976 | bytes 14536704 | tf_op jit(solution)/shard_map/td,vd->tv/dot_general | solution.py:25
  317.8 4.5 %collective-permute-done.42 = f32[2,3,1024]{2,0,1:T(2,128)S(1)} collective-permute-done((f32[2,3,1024]{2,0,1:T(2,128)S(1)}, f32[2,3,1024]{2,0,1:T(2,128)S(1)}, u32[]{:S(2)}, u32[]{:S(2)}) %collective-permute-start.42) | collective-permute-done | bytes 24608 | tf_op jit(solution)/shard_map/ppermute | solution.py:192
  331.3 5.8 %collective-permute-start.45 = (f32[2,3,1024]{2,0,1:T(2,128)S(1)}, f32[2,3,1024]{2,0,1:T(2,128)S(1)}, u32[]{:S(2)}, u32[]{:S(2)}) collective-permute-start(f32[2,3,1024]{2,0,1:T(2,128)S(1)} %pad_maximum_fusion.26), channel_id=1, source_target_pairs={{0,32},{2,34},{4,36},{6,38},{8,40},{10,42},{12,44},{14,46},{16,48}... | collective-permute-start | bytes 73736 | tf_op jit(solution)/shard_map/ppermute | solution.py:192
  (218 shorter events, 109.2 us)
Async XLA Ops:
  7.2 296.5 %all-gather.2.cloned.1.call-start = ((), (), s32[]{:S(2)}) async-start(), calls=%async_computation | async-start | bytes 10485760 | tf_op jit(solution)/shard_map/all_gather | solution.py:170
  8.1 11.7 %collective-permute-start = (bf16[4,4096]{1,0:T(4,128)(2,1)S(1)}, bf16[4,4096]{1,0:T(4,128)(2,1)S(1)}, u32[]{:S(2)}, u32[]{:S(2)}) collective-permute-start(bf16[4,4096]{1,0:T(4,128)(2,1)S(1)} %get-tuple-element.72), channel_id=1, source_target_pairs={{0,1},{1,0},{2,3},{3,2},{4,5},{5,4},{6,7},{7,6},{8,9},{9,8},{10,11... | collective-permute-start | bytes 98312 | tf_op jit(solution)/shard_map/ppermute | solution.py:145
  8.2 84.4 %collective-permute-start.13 = (bf16[4096,172]{0,1:T(8,128)(2,1)}, bf16[4096,172]{0,1:T(8,128)(2,1)}, u32[]{:S(2)}, u32[]{:S(2)}) collective-permute-start(bf16[4096,172]{0,1:T(8,128)(2,1)} %param.23), channel_id=1, source_target_pairs={{1,0},{3,2},{5,4},{7,6},{9,8},{11,10},{13,12},{15,14},{17,16},{19,... | collective-permute-start | bytes 4227080 | tf_op jit(solution)/shard_map/ppermute | solution.py:141
  9.6 86.4 %collective-permute-start.14 = (bf16[4096,172]{0,1:T(8,128)(2,1)}, bf16[4096,172]{0,1:T(8,128)(2,1)}, u32[]{:S(2)}, u32[]{:S(2)}) collective-permute-start(bf16[4096,172]{0,1:T(8,128)(2,1)} %param.26), channel_id=1, source_target_pairs={{0,1},{2,3},{4,5},{6,7},{8,9},{10,11},{12,13},{14,15},{16,17},{18,... | collective-permute-start | bytes 4227080 | tf_op jit(solution)/shard_map/ppermute | solution.py:142
  14.8 82.7 %collective-permute-start.11 = (bf16[4096,172]{0,1:T(8,128)(2,1)}, bf16[4096,172]{0,1:T(8,128)(2,1)}, u32[]{:S(2)}, u32[]{:S(2)}) collective-permute-start(bf16[4096,172]{0,1:T(8,128)(2,1)} %param.22), channel_id=1, source_target_pairs={{1,0},{3,2},{5,4},{7,6},{9,8},{11,10},{13,12},{15,14},{17,16},{19,... | collective-permute-start | bytes 4227080 | tf_op jit(solution)/shard_map/ppermute | solution.py:141
  19.9 9.2 %collective-permute-start.1 = (bf16[1,1,1,1,1,8,2048]{6,5,4,3,2,1,0:T(8,128)(2,1)S(1)}, bf16[1,1,1,1,1,8,2048]{6,5,4,3,2,1,0:T(8,128)(2,1)S(1)}, u32[]{:S(2)}, u32[]{:S(2)}) collective-permute-start(bf16[1,1,1,1,1,8,2048]{6,5,4,3,2,1,0:T(8,128)(2,1)S(1)} %get-tuple-element.69), channel_id=1, source_target_pairs={{0,32},{2,34},{4,36},{6,38},{8,40},{10,42},{12,44},{14,46},{16,48}... | collective-permute-start | bytes 98312 | tf_op jit(solution)/shard_map/ppermute | solution.py:72
  42.3 55.3 %collective-permute-start.12 = (bf16[4096,172]{0,1:T(8,128)(2,1)}, bf16[4096,172]{0,1:T(8,128)(2,1)S(1)}, u32[]{:S(2)}, u32[]{:S(2)}) collective-permute-start(bf16[4096,172]{0,1:T(8,128)(2,1)} %param.25), channel_id=1, source_target_pairs={{0,1},{2,3},{4,5},{6,7},{8,9},{10,11},{12,13},{14,15},{16,17},{18,... | collective-permute-start | bytes 4227080 | tf_op jit(solution)/shard_map/ppermute | solution.py:142
  62.4 8.6 %collective-permute-start.9 = (bf16[2,2,1,1,2,8,2048]{6,5,4,3,2,1,0:T(8,128)(2,1)S(1)}, bf16[2,2,1,1,2,8,2048]{6,5,4,3,2,1,0:T(8,128)(2,1)S(1)}, u32[]{:S(2)}, u32[]{:S(2)}) collective-permute-start(bf16[2,2,1,1,2,8,2048]{6,5,4,3,2,1,0:T(8,128)(2,1)S(1)} %pad_maximum_fusion.12), channel_id=1, source_target_pairs={{0,6},{2,4},{4,2},{6,0},{8,14},{10,12},{12,10},{14,8},{16,22},{18,... | collective-permute-start | bytes 786440 | tf_op jit(solution)/shard_map/ppermute | solution.py:72
  71.0 10.4 %collective-permute-start.5 = (bf16[2,2,2,1,2,8,2048]{6,5,4,3,2,1,0:T(8,128)(2,1)S(1)}, bf16[2,2,2,1,2,8,2048]{6,5,4,3,2,1,0:T(8,128)(2,1)S(1)}, u32[]{:S(2)}, u32[]{:S(2)}) collective-permute-start(bf16[2,2,2,1,2,8,2048]{6,5,4,3,2,1,0:T(8,128)(2,1)S(1)} %pad_maximum_fusion.7), channel_id=1, source_target_pairs={{0,6},{2,4},{4,2},{6,0},{8,14},{10,12},{12,10},{14,8},{16,22},{18,... | collective-permute-start | bytes 1572872 | tf_op jit(solution)/shard_map/ppermute | solution.py:72
  81.4 9.2 %collective-permute-start.10 = (bf16[2,2,1,2,2,8,2048]{6,5,4,3,2,1,0:T(8,128)(2,1)S(1)}, bf16[2,2,1,2,2,8,2048]{6,5,4,3,2,1,0:T(8,128)(2,1)S(1)}, u32[]{:S(2)}, u32[]{:S(2)}) collective-permute-start(bf16[2,2,1,2,2,8,2048]{6,5,4,3,2,1,0:T(8,128)(2,1)S(1)} %pad_maximum_fusion.8), channel_id=1, source_target_pairs={{0,8},{2,10},{4,12},{6,14},{8,0},{10,2},{12,4},{14,6},{16,24},{18,... | collective-permute-start | bytes 1572872 | tf_op jit(solution)/shard_map/ppermute | solution.py:72
  90.6 11.1 %collective-permute-start.15 = (bf16[172,4096]{1,0:T(8,128)(2,1)S(1)}, bf16[172,4096]{1,0:T(8,128)(2,1)S(1)}, u32[]{:S(2)}, u32[]{:S(2)}) collective-permute-start(bf16[172,4096]{1,0:T(8,128)(2,1)S(1)} %copy-done.2), channel_id=1, source_target_pairs={{1,0},{3,2},{5,4},{7,6},{9,8},{11,10},{13,12},{15,14},{17,16},{19,... | collective-permute-start | bytes 4227080 | tf_op jit(solution)/shard_map/ppermute | solution.py:141
  92.6 9.1 %collective-permute-start.16 = (bf16[172,4096]{1,0:T(8,128)(2,1)S(1)}, bf16[172,4096]{1,0:T(8,128)(2,1)S(1)}, u32[]{:S(2)}, u32[]{:S(2)}) collective-permute-start(bf16[172,4096]{1,0:T(8,128)(2,1)S(1)} %copy-done.3), channel_id=1, source_target_pairs={{0,1},{2,3},{4,5},{6,7},{8,9},{10,11},{12,13},{14,15},{16,17},{18,... | collective-permute-start | bytes 4227080 | tf_op jit(solution)/shard_map/ppermute | solution.py:142
  105.0 25.2 %collective-permute-start.17 = (f32[2,2,2,1,2,8,2048]{6,5,4,3,2,1,0:T(8,128)S(1)}, f32[2,2,2,1,2,8,2048]{6,5,4,3,2,1,0:T(8,128)S(1)}, u32[]{:S(2)}, u32[]{:S(2)}) collective-permute-start(f32[2,2,2,1,2,8,2048]{6,5,4,3,2,1,0:T(8,128)S(1)} %slice_select_fusion.1), channel_id=1, source_target_pairs={{0,6},{2,4},{4,2},{6,0},{8,14},{10,12},{12,10},{14,8},{16,22},{18,... | collective-permute-start | bytes 3145736 | tf_op jit(solution)/shard_map/ppermute | solution.py:100
  105.7 25.1 %collective-permute-start.22 = (f32[2,2,1,2,2,8,2048]{6,5,4,3,2,1,0:T(8,128)S(1)}, f32[2,2,1,2,2,8,2048]{6,5,4,3,2,1,0:T(8,128)S(1)}, u32[]{:S(2)}, u32[]{:S(2)}) collective-permute-start(f32[2,2,1,2,2,8,2048]{6,5,4,3,2,1,0:T(8,128)S(1)} %slice_select_fusion), channel_id=1, source_target_pairs={{0,8},{2,10},{4,12},{6,14},{8,0},{10,2},{12,4},{14,6},{16,24},{18,... | collective-permute-start | bytes 3145736 | tf_op jit(solution)/shard_map/ppermute | solution.py:100
  130.5 11.9 %collective-permute-start.18 = (f32[2,2,1,1,2,8,2048]{6,5,4,3,2,1,0:T(8,128)S(1)}, f32[2,2,1,1,2,8,2048]{6,5,4,3,2,1,0:T(8,128)S(1)}, u32[]{:S(2)}, u32[]{:S(2)}) collective-permute-start(f32[2,2,1,1,2,8,2048]{6,5,4,3,2,1,0:T(8,128)S(1)} %slice_select_fusion.3), channel_id=1, source_target_pairs={{0,8},{2,10},{4,12},{6,14},{8,0},{10,2},{12,4},{14,6},{16,24},{18,... | collective-permute-start | bytes 1572872 | tf_op jit(solution)/shard_map/ppermute | solution.py:100
  131.0 13.0 %collective-permute-start.23 = (f32[2,2,1,1,2,8,2048]{6,5,4,3,2,1,0:T(8,128)S(1)}, f32[2,2,1,1,2,8,2048]{6,5,4,3,2,1,0:T(8,128)S(1)}, u32[]{:S(2)}, u32[]{:S(2)}) collective-permute-start(f32[2,2,1,1,2,8,2048]{6,5,4,3,2,1,0:T(8,128)S(1)} %slice_select_fusion.2), channel_id=1, source_target_pairs={{0,6},{2,4},{4,2},{6,0},{8,14},{10,12},{12,10},{14,8},{16,22},{18,... | collective-permute-start | bytes 1572872 | tf_op jit(solution)/shard_map/ppermute | solution.py:100
  144.1 15.8 %collective-permute-start.24 = (f32[2,1,1,1,2,8,2048]{6,5,4,3,2,1,0:T(8,128)S(1)}, f32[2,1,1,1,2,8,2048]{6,5,4,3,2,1,0:T(8,128)S(1)}, u32[]{:S(2)}, u32[]{:S(2)}) collective-permute-start(f32[2,1,1,1,2,8,2048]{6,5,4,3,2,1,0:T(8,128)S(1)} %slice_select_fusion.4), channel_id=1, source_target_pairs={{0,16},{2,18},{4,20},{6,22},{8,24},{10,26},{12,28},{14,30},{16,0},... | collective-permute-start | bytes 786440 | tf_op jit(solution)/shard_map/ppermute | solution.py:100
  149.0 12.4 %collective-permute-start.20 = (f32[2,1,1,1,1,8,2048]{6,5,4,3,2,1,0:T(8,128)S(1)}, f32[2,1,1,1,1,8,2048]{6,5,4,3,2,1,0:T(8,128)S(1)}, u32[]{:S(2)}, u32[]{:S(2)}) collective-permute-start(f32[2,1,1,1,1,8,2048]{6,5,4,3,2,1,0:T(8,128)S(1)} %slice_select_fusion.7), channel_id=1, source_target_pairs={{0,16},{2,18},{4,20},{6,22},{8,24},{10,26},{12,28},{14,30},{16,0},... | collective-permute-start | bytes 393224 | tf_op jit(solution)/shard_map/ppermute | solution.py:100
  161.5 9.8 %collective-permute-start.21 = (f32[1,1,1,1,1,8,2048]{6,5,4,3,2,1,0:T(8,128)S(1)}, f32[1,1,1,1,1,8,2048]{6,5,4,3,2,1,0:T(8,128)S(1)}, u32[]{:S(2)}, u32[]{:S(2)}) collective-permute-start(f32[1,1,1,1,1,8,2048]{6,5,4,3,2,1,0:T(8,128)S(1)} %slice_select_fusion.9), channel_id=1, source_target_pairs={{0,32},{2,34},{4,36},{6,38},{8,40},{10,42},{12,44},{14,46},{16,48}... | collective-permute-start | bytes 196616 | tf_op jit(solution)/shard_map/ppermute | solution.py:100
  165.1 8.5 %collective-permute-start.26 = (f32[1,1,1,1,1,8,2048]{6,5,4,3,2,1,0:T(8,128)S(1)}, f32[1,1,1,1,1,8,2048]{6,5,4,3,2,1,0:T(8,128)S(1)}, u32[]{:S(2)}, u32[]{:S(2)}) collective-permute-start(f32[1,1,1,1,1,8,2048]{6,5,4,3,2,1,0:T(8,128)S(1)} %slice_select_fusion.8), channel_id=1, source_target_pairs={{0,32},{2,34},{4,36},{6,38},{8,40},{10,42},{12,44},{14,46},{16,48}... | collective-permute-start | bytes 196616 | tf_op jit(solution)/shard_map/ppermute | solution.py:100
  199.0 9.3 %collective-permute-start.36 = (bf16[2,2,1,1,2,8,2048]{6,5,4,3,2,1,0:T(8,128)(2,1)S(1)}, bf16[2,2,1,1,2,8,2048]{6,5,4,3,2,1,0:T(8,128)(2,1)S(1)}, u32[]{:S(2)}, u32[]{:S(2)}) collective-permute-start(bf16[2,2,1,1,2,8,2048]{6,5,4,3,2,1,0:T(8,128)(2,1)S(1)} %pad_maximum_fusion.14), channel_id=1, source_target_pairs={{0,6},{2,4},{4,2},{6,0},{8,14},{10,12},{12,10},{14,8},{16,22},{18,... | collective-permute-start | bytes 786440 | tf_op jit(solution)/shard_map/ppermute | solution.py:72
  205.3 10.5 %collective-permute-start.32 = (bf16[2,2,2,1,2,8,2048]{6,5,4,3,2,1,0:T(8,128)(2,1)S(1)}, bf16[2,2,2,1,2,8,2048]{6,5,4,3,2,1,0:T(8,128)(2,1)S(1)}, u32[]{:S(2)}, u32[]{:S(2)}) collective-permute-start(bf16[2,2,2,1,2,8,2048]{6,5,4,3,2,1,0:T(8,128)(2,1)S(1)} %pad_maximum_fusion.9), channel_id=1, source_target_pairs={{0,6},{2,4},{4,2},{6,0},{8,14},{10,12},{12,10},{14,8},{16,22},{18,... | collective-permute-start | bytes 1572872 | tf_op jit(solution)/shard_map/ppermute | solution.py:72
  208.5 9.3 %collective-permute-start.37 = (bf16[2,2,1,2,2,8,2048]{6,5,4,3,2,1,0:T(8,128)(2,1)S(1)}, bf16[2,2,1,2,2,8,2048]{6,5,4,3,2,1,0:T(8,128)(2,1)S(1)}, u32[]{:S(2)}, u32[]{:S(2)}) collective-permute-start(bf16[2,2,1,2,2,8,2048]{6,5,4,3,2,1,0:T(8,128)(2,1)S(1)} %pad_maximum_fusion.10), channel_id=1, source_target_pairs={{0,8},{2,10},{4,12},{6,14},{8,0},{10,2},{12,4},{14,6},{16,24},{18,... | collective-permute-start | bytes 1572872 | tf_op jit(solution)/shard_map/ppermute | solution.py:72
  221.0 8.5 %collective-permute-start.38 = (bf16[250,4096]{1,0:T(8,128)(2,1)S(1)}, bf16[250,4096]{1,0:T(8,128)(2,1)}, u32[]{:S(2)}, u32[]{:S(2)}) collective-permute-start(bf16[250,4096]{1,0:T(8,128)(2,1)S(1)} %copy-done), channel_id=1, source_target_pairs={{1,0},{3,2},{5,4},{7,6},{9,8},{11,10},{13,12},{15,14},{17,16},{19,... | collective-permute-start | bytes 6144008 | tf_op jit(solution)/shard_map/ppermute | solution.py:174
  (38 other events, 387.0 us)
Sparse Core Ops, SparseCore 0:
  219.6 84.0 all-gather.1

commit v2 on v0

--- a/solution.py
+++ b/solution.py
@@ -158,6 +158,7 @@
     hidden = (jax.nn.silu(gate) * upper).astype(jnp.bfloat16)
     partial = jnp.dot(hidden, down, preferred_element_type=jnp.float32)
     mixed = scatter_halving(partial)
+    mixed, pol_head, ref_head = lax.optimization_barrier((mixed, pol_head, ref_head))
     out = (pair_rows.astype(jnp.float32) + mixed).astype(jnp.bfloat16)
     final = gather_doubling(rms_rows(out, jnp.where(first, pol_final_gain, ref_final_gain)))
     mine_out = lax.dynamic_slice_in_dim(out, core * rows, rows, axis=0)

time: 322 us -> 322 us (level)
  no operation moved by 1% of the time
where the time goes in v2:
time: 322 us
  waiting for transfers between devices  214 us (66%)
  starting transfers between devices  55.5 us (17%)
  other arithmetic  16.5 us (5%)
  between operations  14.8 us (5%)
  matrix products  14 us (4%)
  local copies, waits for them, and re-layouts  7.67 us (2%)
    all_gather x1, waiting for transfers between devices, per_device(): every = lax.all_gather(final, 'grp', axis=0, tiled=True)  74.4 us
    ppermute x20, waiting for transfers between devices, gather_doubling(): lax.ppermute(held, 'zx', [(i, i ^ partner_mask(bit)) for i in range(size)])  62.4 us
    ppermute x10, waiting for transfers between devices, scatter_halving(): lax.ppermute(jnp.where(low, upper, lower), 'zx', [(i, i ^ partner_mask(bi...  52.9 us
    ppermute x20, starting transfers between devices, gather_doubling(): lax.ppermute(held, 'zx', [(i, i ^ partner_mask(bit)) for i in range(size)])  30.3 us
    ppermute x7, waiting for transfers between devices, per_device(): lax.ppermute(state, axis, [(i, i ^ partner_mask(bit)) for i in range(size)])  18.3 us
    ppermute x7, starting transfers between devices, per_device(): lax.ppermute(state, axis, [(i, i ^ partner_mask(bit)) for i in range(size)])  15.5 us
    ppermute x10, starting transfers between devices, scatter_halving(): lax.ppermute(jnp.where(low, upper, lower), 'zx', [(i, i ^ partner_mask(bi...  8.42 us
    dot_general x1, matrix products, vocab_terms(): jnp.einsum('td,vd->tv', token_rows, head_rows, preferred_element_type=jnp...  7.62 us
  transfers between devices with their start and end apart: 45, of which 36 were waited for; matrix products, arithmetic and copies ran while one was open for 6% of the time, Pallas kernels for 0%

profile of v2, /device:TPU:6, one launch (start us, length us, event | category | flops | bytes accessed | tf_op | source)
XLA Modules:
  0.0 322.0 jit_solution(11579627259589519289)
XLA Ops:
  8.1 4.3 %conditional.1 = (bf16[172,4096]{1,0:T(8,128)(2,1)S(1)}, bf16[4096,172]{0,1:T(8,128)(2,1)}, bf16[4096,172]{0,1:T(8,128)(2,1)}) conditional(s32[]{:T(128)} %convert_element_type.38, (bf16[4096,172]{0,1:T(8,128)(2,1)}, bf16[4096,172]{0,1:T(8,128)(2,1)}, bf16[172,4096]{1,0:T(8,128)(2,1)}) %tuple.15, (bf16[4096,172]{0,1:T(8,128)(2,1)}, ...), branch_computations={%region_1.0_spmd, %region_2.3_spmd} | conditional | bytes 19726416 | solution.py:141
  13.4 3.9 %broadcast_select_fusion.3 = (bf16[4096,172]{0,1:T(8,128)(2,1)}, bf16[4096,172]{0,1:T(8,128)(2,1)}) fusion(bf16[4096,172]{0,1:T(8,128)(2,1)} %param.25, bf16[4096,172]{0,1:T(8,128)(2,1)} %param.28, pred[]{:T(512)S(6)} %eq.28, bf16[4096,172]{0,1:T(8,128)(2,1)} %param.24, bf16[4096,172]{0,1:T(8,128)(2,1)} %param.27), kind=kLoop, calls=%fused_computation.30 | loop fusion | flops 1409024 | bytes 8454145 | tf_op jit(solution)/shard_map/jit(_where)/select_n | solution.py:151
  17.4 7.3 %collective-permute-start.1 = (bf16[1,1,1,1,1,8,2048]{6,5,4,3,2,1,0:T(8,128)(2,1)S(1)}, bf16[1,1,1,1,1,8,2048]{6,5,4,3,2,1,0:T(8,128)(2,1)S(1)}, u32[]{:S(2)}, u32[]{:S(2)}) collective-permute-start(bf16[1,1,1,1,1,8,2048]{6,5,4,3,2,1,0:T(8,128)(2,1)S(1)} %get-tuple-element.121), channel_id=1, source_target_pairs={{0,32},{2,34},{4,36},{6,38},{8,40},{10,42},{12,44},{14,46},{16,48}... | collective-permute-start | bytes 98312 | tf_op jit(solution)/shard_map/ppermute | solution.py:72
  26.6 6.3 %collective-permute-done.6 = bf16[1,1,1,1,1,8,2048]{6,5,4,3,2,1,0:T(8,128)(2,1)S(1)} collective-permute-done((bf16[1,1,1,1,1,8,2048]{6,5,4,3,2,1,0:T(8,128)(2,1)S(1)}, bf16[1,1,1,1,1,8,2048]{6,5,4,3,2,1,0:T(8,128)(2,1)S(1)}, u32[]{:S(2)}, u32[]{:S(2)}) %collective-permute-start.6) | collective-permute-done | bytes 32800 | tf_op jit(solution)/shard_map/ppermute | solution.py:72
  35.2 3.6 %collective-permute-done.2 = bf16[2,1,1,1,1,8,2048]{6,5,4,3,2,1,0:T(8,128)(2,1)S(1)} collective-permute-done((bf16[2,1,1,1,1,8,2048]{6,5,4,3,2,1,0:T(8,128)(2,1)S(1)}, bf16[2,1,1,1,1,8,2048]{6,5,4,3,2,1,0:T(8,128)(2,1)S(1)}, u32[]{:S(2)}, u32[]{:S(2)}) %collective-permute-start.2) | collective-permute-done | bytes 65568 | tf_op jit(solution)/shard_map/ppermute | solution.py:72
  51.5 6.2 %collective-permute-done.9 = bf16[2,2,1,1,2,8,2048]{6,5,4,3,2,1,0:T(8,128)(2,1)S(1)} collective-permute-done((bf16[2,2,1,1,2,8,2048]{6,5,4,3,2,1,0:T(8,128)(2,1)S(1)}, bf16[2,2,1,1,2,8,2048]{6,5,4,3,2,1,0:T(8,128)(2,1)S(1)}, u32[]{:S(2)}, u32[]{:S(2)}) %collective-permute-start.9) | collective-permute-done | bytes 262176 | tf_op jit(solution)/shard_map/ppermute | solution.py:72
  58.6 6.7 %collective-permute-done.5 = bf16[2,2,2,1,2,8,2048]{6,5,4,3,2,1,0:T(8,128)(2,1)S(1)} collective-permute-done((bf16[2,2,2,1,2,8,2048]{6,5,4,3,2,1,0:T(8,128)(2,1)S(1)}, bf16[2,2,2,1,2,8,2048]{6,5,4,3,2,1,0:T(8,128)(2,1)S(1)}, u32[]{:S(2)}, u32[]{:S(2)}) %collective-permute-start.5) | collective-permute-done | bytes 524320 | tf_op jit(solution)/shard_map/ppermute | solution.py:72
  69.1 3.7 %fusion = f32[256,688]{0,1:T(8,128)S(1)} fusion(bf16[4096,172]{0,1:T(8,128)(2,1)} %collective-permute-done.12, bf16[4096,172]{0,1:T(8,128)(2,1)S(1)} %copy-done.7, bf16[4096,172]{0,1:T(8,128)(2,1)} %collective-permute-done.11, bf16[4096,172]{0,1:T(8,128)(2,1)S(1)} %copy-done.8, f32[4096]{0:T(1024)S(1)} %select_convert_fusion.1, f32[256]{0:T(256)S(1)} %add_rsqrt_fusion, ...), kind=kOutput, calls=%fused_computation | convolution fusion | flops 1472724992 | bytes 8455168 | tf_op jit(solution)/shard_map/dot_general | solution.py:156
  78.2 19.1 %collective-permute-done.14 = f32[2,2,2,1,2,8,2048]{6,5,4,3,2,1,0:T(8,128)S(1)} collective-permute-done((f32[2,2,2,1,2,8,2048]{6,5,4,3,2,1,0:T(8,128)S(1)}, f32[2,2,2,1,2,8,2048]{6,5,4,3,2,1,0:T(8,128)S(1)}, u32[]{:S(2)}, u32[]{:S(2)}) %collective-permute-start.14) | collective-permute-done | bytes 1048608 | tf_op jit(solution)/shard_map/ppermute | solution.py:100
  98.6 3.6 %collective-permute-done.19 = f32[2,2,1,2,2,8,2048]{6,5,4,3,2,1,0:T(8,128)S(1)} collective-permute-done((f32[2,2,1,2,2,8,2048]{6,5,4,3,2,1,0:T(8,128)S(1)}, f32[2,2,1,2,2,8,2048]{6,5,4,3,2,1,0:T(8,128)S(1)}, u32[]{:S(2)}, u32[]{:S(2)}) %collective-permute-start.19) | collective-permute-done | bytes 1048608 | tf_op jit(solution)/shard_map/ppermute | solution.py:100
  102.7 6.9 %collective-permute-done.15 = f32[2,2,1,1,2,8,2048]{6,5,4,3,2,1,0:T(8,128)S(1)} collective-permute-done((f32[2,2,1,1,2,8,2048]{6,5,4,3,2,1,0:T(8,128)S(1)}, f32[2,2,1,1,2,8,2048]{6,5,4,3,2,1,0:T(8,128)S(1)}, u32[]{:S(2)}, u32[]{:S(2)}) %collective-permute-start.15) | collective-permute-done | bytes 524320 | tf_op jit(solution)/shard_map/ppermute | solution.py:100
  116.8 8.3 %collective-permute-done.21 = f32[2,1,1,1,2,8,2048]{6,5,4,3,2,1,0:T(8,128)S(1)} collective-permute-done((f32[2,1,1,1,2,8,2048]{6,5,4,3,2,1,0:T(8,128)S(1)}, f32[2,1,1,1,2,8,2048]{6,5,4,3,2,1,0:T(8,128)S(1)}, u32[]{:S(2)}, u32[]{:S(2)}) %collective-permute-start.21) | collective-permute-done | bytes 262176 | tf_op jit(solution)/shard_map/ppermute | solution.py:100
  147.0 3.4 %collective-permute-done.30 = bf16[1,1,1,1,1,8,2048]{6,5,4,3,2,1,0:T(8,128)(2,1)S(1)} collective-permute-done((bf16[1,1,1,1,1,8,2048]{6,5,4,3,2,1,0:T(8,128)(2,1)S(1)}, bf16[1,1,1,1,1,8,2048]{6,5,4,3,2,1,0:T(8,128)(2,1)S(1)}, u32[]{:S(2)}, u32[]{:S(2)}) %collective-permute-start.30) | collective-permute-done | bytes 32800 | tf_op jit(solution)/shard_map/ppermute | solution.py:72
  151.7 5.9 %collective-permute-done.26 = bf16[2,1,1,1,1,8,2048]{6,5,4,3,2,1,0:T(8,128)(2,1)S(1)} collective-permute-done((bf16[2,1,1,1,1,8,2048]{6,5,4,3,2,1,0:T(8,128)(2,1)S(1)}, bf16[2,1,1,1,1,8,2048]{6,5,4,3,2,1,0:T(8,128)(2,1)S(1)}, u32[]{:S(2)}, u32[]{:S(2)}) %collective-permute-start.26) | collective-permute-done | bytes 65568 | tf_op jit(solution)/shard_map/ppermute | solution.py:72
  159.0 3.7 %collective-permute-done.27 = bf16[2,2,1,1,1,8,2048]{6,5,4,3,2,1,0:T(8,128)(2,1)S(1)} collective-permute-done((bf16[2,2,1,1,1,8,2048]{6,5,4,3,2,1,0:T(8,128)(2,1)S(1)}, bf16[2,2,1,1,1,8,2048]{6,5,4,3,2,1,0:T(8,128)(2,1)S(1)}, u32[]{:S(2)}, u32[]{:S(2)}) %collective-permute-start.27) | collective-permute-done | bytes 131104 | tf_op jit(solution)/shard_map/ppermute | solution.py:72
  167.3 3.4 %collective-permute-done.28 = bf16[2,2,1,1,2,8,2048]{6,5,4,3,2,1,0:T(8,128)(2,1)S(1)} collective-permute-done((bf16[2,2,1,1,2,8,2048]{6,5,4,3,2,1,0:T(8,128)(2,1)S(1)}, bf16[2,2,1,1,2,8,2048]{6,5,4,3,2,1,0:T(8,128)(2,1)S(1)}, u32[]{:S(2)}, u32[]{:S(2)}) %collective-permute-start.28) | collective-permute-done | bytes 262176 | tf_op jit(solution)/shard_map/ppermute | solution.py:72
  170.8 3.3 %collective-permute-start.29 = (bf16[2,2,2,1,2,8,2048]{6,5,4,3,2,1,0:T(8,128)(2,1)S(1)}, bf16[2,2,2,1,2,8,2048]{6,5,4,3,2,1,0:T(8,128)(2,1)S(1)}, u32[]{:S(2)}, u32[]{:S(2)}) collective-permute-start(bf16[2,2,2,1,2,8,2048]{6,5,4,3,2,1,0:T(8,128)(2,1)S(1)} %pad_maximum_fusion.9), channel_id=1, source_target_pairs={{0,6},{2,4},{4,2},{6,0},{8,14},{10,12},{12,10},{14,8},{16,22},{18,... | collective-permute-start | bytes 1572872 | tf_op jit(solution)/shard_map/ppermute | solution.py:72
  174.3 7.0 %collective-permute-done.29 = bf16[2,2,2,1,2,8,2048]{6,5,4,3,2,1,0:T(8,128)(2,1)S(1)} collective-permute-done((bf16[2,2,2,1,2,8,2048]{6,5,4,3,2,1,0:T(8,128)(2,1)S(1)}, bf16[2,2,2,1,2,8,2048]{6,5,4,3,2,1,0:T(8,128)(2,1)S(1)}, u32[]{:S(2)}, u32[]{:S(2)}) %collective-permute-start.29) | collective-permute-done | bytes 524320 | tf_op jit(solution)/shard_map/ppermute | solution.py:72
  186.8 3.9 %broadcast_select_fusion.1 = (bf16[250,4096]{1,0:T(8,128)(2,1)}, bf16[250,4096]{1,0:T(8,128)(2,1)}) fusion(bf16[250,4096]{1,0:T(8,128)(2,1)S(1)} %copy-done.6, bf16[250,4096]{1,0:T(8,128)(2,1)} %param.31, pred[]{:T(512)S(6)} %eq.28), kind=kLoop, calls=%fused_computation.26 | loop fusion | flops 2048000 | bytes 8192001 | tf_op jit(solution)/shard_map/jit(_where)/select_n | solution.py:109
  190.8 4.3 %collective-permute-done.35 = bf16[250,4096]{1,0:T(8,128)(2,1)S(1)} collective-permute-done((bf16[250,4096]{1,0:T(8,128)(2,1)}, bf16[250,4096]{1,0:T(8,128)(2,1)S(1)}, u32[]{:S(2)}, u32[]{:S(2)}) %collective-permute-start.35) | collective-permute-done | bytes 2048032 | tf_op jit(solution)/shard_map/ppermute | solution.py:171
  195.1 74.4 %all-gather.2.cloned.1.call-done = bf16[1024,4096]{1,0:T(8,128)(2,1)} async-done(((bf16[256,4096]{1,0:T(8,128)(2,1)}), bf16[1024,4096]{1,0:T(8,128)(2,1)}) %all-gather.2.cloned.1.call-update) | async-done | bytes 8388624 | tf_op jit(solution)/shard_map/all_gather | solution.py:169
  269.5 7.6 %fusion.47 = (f32[1024]{0:T(1024)S(1)}, f32[1024,500]{0,1:T(8,128)S(1)}) fusion(bf16[1024,4096]{1,0:T(8,128)(2,1)} %all-gather.2.cloned.1.call-done, bf16[250,4096]{1,0:T(8,128)(2,1)S(1)} %collective-permute-done.35, bf16[250,4096]{1,0:T(8,128)(2,1)} %get-tuple-element.69), kind=kOutput, calls=%fused_computation.215 | convolution fusion | flops 4203006976 | bytes 14536704 | tf_op jit(solution)/shard_map/td,vd->tv/dot_general | solution.py:25
  283.7 4.5 %collective-permute-done.38 = f32[2,3,1024]{2,0,1:T(2,128)S(1)} collective-permute-done((f32[2,3,1024]{2,0,1:T(2,128)S(1)}, f32[2,3,1024]{2,0,1:T(2,128)S(1)}, u32[]{:S(2)}, u32[]{:S(2)}) %collective-permute-start.38) | collective-permute-done | bytes 24608 | tf_op jit(solution)/shard_map/ppermute | solution.py:187
  297.4 5.8 %collective-permute-start.41 = (f32[2,3,1024]{2,0,1:T(2,128)S(1)}, f32[2,3,1024]{2,0,1:T(2,128)S(1)}, u32[]{:S(2)}, u32[]{:S(2)}) collective-permute-start(f32[2,3,1024]{2,0,1:T(2,128)S(1)} %pad_maximum_fusion.27), channel_id=1, source_target_pairs={{0,32},{2,34},{4,36},{6,38},{8,40},{10,42},{12,44},{14,46},{16,48}... | collective-permute-start | bytes 73736 | tf_op jit(solution)/shard_map/ppermute | solution.py:187
  (211 shorter events, 104.5 us)
Async XLA Ops:
  7.2 262.3 %all-gather.2.cloned.1.call-start = ((), (), s32[]{:S(2)}) async-start(), calls=%async_computation | async-start | bytes 10485760 | tf_op jit(solution)/shard_map/all_gather | solution.py:169
  8.0 9.3 %collective-permute-start = (bf16[4,4096]{1,0:T(4,128)(2,1)S(1)}, bf16[4,4096]{1,0:T(4,128)(2,1)S(1)}, u32[]{:S(2)}, u32[]{:S(2)}) collective-permute-start(bf16[4,4096]{1,0:T(4,128)(2,1)S(1)} %get-tuple-element.124), channel_id=1, source_target_pairs={{0,1},{1,0},{2,3},{3,2},{4,5},{5,4},{6,7},{7,6},{8,9},{9,8},{10,11... | collective-permute-start | bytes 98312 | tf_op jit(solution)/shard_map/ppermute | solution.py:143
  12.4 55.5 %collective-permute-start.11 = (bf16[4096,172]{0,1:T(8,128)(2,1)}, bf16[4096,172]{0,1:T(8,128)(2,1)}, u32[]{:S(2)}, u32[]{:S(2)}) collective-permute-start(bf16[4096,172]{0,1:T(8,128)(2,1)} %get-tuple-element.51), channel_id=1, source_target_pairs={{0,1},{1,0},{2,3},{3,2},{4,5},{5,4},{6,7},{7,6},{8,9},{9,8},{10,11... | collective-permute-start | bytes 4227080 | tf_op jit(solution)/shard_map/ppermute | solution.py:141
  12.9 55.0 %collective-permute-start.12 = (bf16[4096,172]{0,1:T(8,128)(2,1)}, bf16[4096,172]{0,1:T(8,128)(2,1)}, u32[]{:S(2)}, u32[]{:S(2)}) collective-permute-start(bf16[4096,172]{0,1:T(8,128)(2,1)} %get-tuple-element.52), channel_id=1, source_target_pairs={{0,1},{1,0},{2,3},{3,2},{4,5},{5,4},{6,7},{7,6},{8,9},{9,8},{10,11... | collective-permute-start | bytes 4227080 | tf_op jit(solution)/shard_map/ppermute | solution.py:141
  12.9 59.8 %collective-permute-start.13 = (bf16[172,4096]{1,0:T(8,128)(2,1)S(1)}, bf16[172,4096]{1,0:T(8,128)(2,1)}, u32[]{:S(2)}, u32[]{:S(2)}) collective-permute-start(bf16[172,4096]{1,0:T(8,128)(2,1)S(1)} %get-tuple-element.23), channel_id=1, source_target_pairs={{0,1},{1,0},{2,3},{3,2},{4,5},{5,4},{6,7},{7,6},{8,9},{9,8},{10,11... | collective-permute-start | bytes 4227080 | tf_op jit(solution)/shard_map/ppermute | solution.py:141
  17.4 9.2 %collective-permute-start.1 = (bf16[1,1,1,1,1,8,2048]{6,5,4,3,2,1,0:T(8,128)(2,1)S(1)}, bf16[1,1,1,1,1,8,2048]{6,5,4,3,2,1,0:T(8,128)(2,1)S(1)}, u32[]{:S(2)}, u32[]{:S(2)}) collective-permute-start(bf16[1,1,1,1,1,8,2048]{6,5,4,3,2,1,0:T(8,128)(2,1)S(1)} %get-tuple-element.121), channel_id=1, source_target_pairs={{0,32},{2,34},{4,36},{6,38},{8,40},{10,42},{12,44},{14,46},{16,48}... | collective-permute-start | bytes 98312 | tf_op jit(solution)/shard_map/ppermute | solution.py:72
  24.7 8.2 %collective-permute-start.6 = (bf16[1,1,1,1,1,8,2048]{6,5,4,3,2,1,0:T(8,128)(2,1)S(1)}, bf16[1,1,1,1,1,8,2048]{6,5,4,3,2,1,0:T(8,128)(2,1)S(1)}, u32[]{:S(2)}, u32[]{:S(2)}) collective-permute-start(bf16[1,1,1,1,1,8,2048]{6,5,4,3,2,1,0:T(8,128)(2,1)S(1)} %get-tuple-element.122), channel_id=1, source_target_pairs={{0,32},{2,34},{4,36},{6,38},{8,40},{10,42},{12,44},{14,46},{16,48}... | collective-permute-start | bytes 98312 | tf_op jit(solution)/shard_map/ppermute | solution.py:72
  47.2 10.4 %collective-permute-start.9 = (bf16[2,2,1,1,2,8,2048]{6,5,4,3,2,1,0:T(8,128)(2,1)S(1)}, bf16[2,2,1,1,2,8,2048]{6,5,4,3,2,1,0:T(8,128)(2,1)S(1)}, u32[]{:S(2)}, u32[]{:S(2)}) collective-permute-start(bf16[2,2,1,1,2,8,2048]{6,5,4,3,2,1,0:T(8,128)(2,1)S(1)} %pad_maximum_fusion.12), channel_id=1, source_target_pairs={{0,6},{2,4},{4,2},{6,0},{8,14},{10,12},{12,10},{14,8},{16,22},{18,... | collective-permute-start | bytes 786440 | tf_op jit(solution)/shard_map/ppermute | solution.py:72
  50.6 14.8 %collective-permute-start.5 = (bf16[2,2,2,1,2,8,2048]{6,5,4,3,2,1,0:T(8,128)(2,1)S(1)}, bf16[2,2,2,1,2,8,2048]{6,5,4,3,2,1,0:T(8,128)(2,1)S(1)}, u32[]{:S(2)}, u32[]{:S(2)}) collective-permute-start(bf16[2,2,2,1,2,8,2048]{6,5,4,3,2,1,0:T(8,128)(2,1)S(1)} %pad_maximum_fusion.7), channel_id=1, source_target_pairs={{0,6},{2,4},{4,2},{6,0},{8,14},{10,12},{12,10},{14,8},{16,22},{18,... | collective-permute-start | bytes 1572872 | tf_op jit(solution)/shard_map/ppermute | solution.py:72
  57.7 9.4 %collective-permute-start.10 = (bf16[2,2,1,2,2,8,2048]{6,5,4,3,2,1,0:T(8,128)(2,1)S(1)}, bf16[2,2,1,2,2,8,2048]{6,5,4,3,2,1,0:T(8,128)(2,1)S(1)}, u32[]{:S(2)}, u32[]{:S(2)}) collective-permute-start(bf16[2,2,1,2,2,8,2048]{6,5,4,3,2,1,0:T(8,128)(2,1)S(1)} %pad_maximum_fusion.8), channel_id=1, source_target_pairs={{0,8},{2,10},{4,12},{6,14},{8,0},{10,2},{12,4},{14,6},{16,24},{18,... | collective-permute-start | bytes 1572872 | tf_op jit(solution)/shard_map/ppermute | solution.py:72
  76.1 21.2 %collective-permute-start.14 = (f32[2,2,2,1,2,8,2048]{6,5,4,3,2,1,0:T(8,128)S(1)}, f32[2,2,2,1,2,8,2048]{6,5,4,3,2,1,0:T(8,128)S(1)}, u32[]{:S(2)}, u32[]{:S(2)}) collective-permute-start(f32[2,2,2,1,2,8,2048]{6,5,4,3,2,1,0:T(8,128)S(1)} %slice_select_fusion.1), channel_id=1, source_target_pairs={{0,6},{2,4},{4,2},{6,0},{8,14},{10,12},{12,10},{14,8},{16,22},{18,... | collective-permute-start | bytes 3145736 | tf_op jit(solution)/shard_map/ppermute | solution.py:100
  77.4 24.9 %collective-permute-start.19 = (f32[2,2,1,2,2,8,2048]{6,5,4,3,2,1,0:T(8,128)S(1)}, f32[2,2,1,2,2,8,2048]{6,5,4,3,2,1,0:T(8,128)S(1)}, u32[]{:S(2)}, u32[]{:S(2)}) collective-permute-start(f32[2,2,1,2,2,8,2048]{6,5,4,3,2,1,0:T(8,128)S(1)} %slice_select_fusion), channel_id=1, source_target_pairs={{0,8},{2,10},{4,12},{6,14},{8,0},{10,2},{12,4},{14,6},{16,24},{18,... | collective-permute-start | bytes 3145736 | tf_op jit(solution)/shard_map/ppermute | solution.py:100
  97.6 11.9 %collective-permute-start.15 = (f32[2,2,1,1,2,8,2048]{6,5,4,3,2,1,0:T(8,128)S(1)}, f32[2,2,1,1,2,8,2048]{6,5,4,3,2,1,0:T(8,128)S(1)}, u32[]{:S(2)}, u32[]{:S(2)}) collective-permute-start(f32[2,2,1,1,2,8,2048]{6,5,4,3,2,1,0:T(8,128)S(1)} %slice_select_fusion.3), channel_id=1, source_target_pairs={{0,8},{2,10},{4,12},{6,14},{8,0},{10,2},{12,4},{14,6},{16,24},{18,... | collective-permute-start | bytes 1572872 | tf_op jit(solution)/shard_map/ppermute | solution.py:100
  102.6 10.5 %collective-permute-start.20 = (f32[2,2,1,1,2,8,2048]{6,5,4,3,2,1,0:T(8,128)S(1)}, f32[2,2,1,1,2,8,2048]{6,5,4,3,2,1,0:T(8,128)S(1)}, u32[]{:S(2)}, u32[]{:S(2)}) collective-permute-start(f32[2,2,1,1,2,8,2048]{6,5,4,3,2,1,0:T(8,128)S(1)} %slice_select_fusion.2), channel_id=1, source_target_pairs={{0,6},{2,4},{4,2},{6,0},{8,14},{10,12},{12,10},{14,8},{16,22},{18,... | collective-permute-start | bytes 1572872 | tf_op jit(solution)/shard_map/ppermute | solution.py:100
  113.2 11.9 %collective-permute-start.21 = (f32[2,1,1,1,2,8,2048]{6,5,4,3,2,1,0:T(8,128)S(1)}, f32[2,1,1,1,2,8,2048]{6,5,4,3,2,1,0:T(8,128)S(1)}, u32[]{:S(2)}, u32[]{:S(2)}) collective-permute-start(f32[2,1,1,1,2,8,2048]{6,5,4,3,2,1,0:T(8,128)S(1)} %slice_select_fusion.4), channel_id=1, source_target_pairs={{0,16},{2,18},{4,20},{6,22},{8,24},{10,26},{12,28},{14,30},{16,0},... | collective-permute-start | bytes 786440 | tf_op jit(solution)/shard_map/ppermute | solution.py:100
  116.2 10.4 %collective-permute-start.17 = (f32[2,1,1,1,1,8,2048]{6,5,4,3,2,1,0:T(8,128)S(1)}, f32[2,1,1,1,1,8,2048]{6,5,4,3,2,1,0:T(8,128)S(1)}, u32[]{:S(2)}, u32[]{:S(2)}) collective-permute-start(f32[2,1,1,1,1,8,2048]{6,5,4,3,2,1,0:T(8,128)S(1)} %slice_select_fusion.7), channel_id=1, source_target_pairs={{0,16},{2,18},{4,20},{6,22},{8,24},{10,26},{12,28},{14,30},{16,0},... | collective-permute-start | bytes 393224 | tf_op jit(solution)/shard_map/ppermute | solution.py:100
  126.7 8.7 %collective-permute-start.18 = (f32[1,1,1,1,1,8,2048]{6,5,4,3,2,1,0:T(8,128)S(1)}, f32[1,1,1,1,1,8,2048]{6,5,4,3,2,1,0:T(8,128)S(1)}, u32[]{:S(2)}, u32[]{:S(2)}) collective-permute-start(f32[1,1,1,1,1,8,2048]{6,5,4,3,2,1,0:T(8,128)S(1)} %slice_select_fusion.9), channel_id=1, source_target_pairs={{0,32},{2,34},{4,36},{6,38},{8,40},{10,42},{12,44},{14,46},{16,48}... | collective-permute-start | bytes 196616 | tf_op jit(solution)/shard_map/ppermute | solution.py:100
  130.2 8.5 %collective-permute-start.23 = (f32[1,1,1,1,1,8,2048]{6,5,4,3,2,1,0:T(8,128)S(1)}, f32[1,1,1,1,1,8,2048]{6,5,4,3,2,1,0:T(8,128)S(1)}, u32[]{:S(2)}, u32[]{:S(2)}) collective-permute-start(f32[1,1,1,1,1,8,2048]{6,5,4,3,2,1,0:T(8,128)S(1)} %slice_select_fusion.8), channel_id=1, source_target_pairs={{0,32},{2,34},{4,36},{6,38},{8,40},{10,42},{12,44},{14,46},{16,48}... | collective-permute-start | bytes 196616 | tf_op jit(solution)/shard_map/ppermute | solution.py:100
  139.0 8.0 %collective-permute-start.25 = (bf16[1,1,1,1,1,8,2048]{6,5,4,3,2,1,0:T(8,128)(2,1)S(1)}, bf16[1,1,1,1,1,8,2048]{6,5,4,3,2,1,0:T(8,128)(2,1)S(1)}, u32[]{:S(2)}, u32[]{:S(2)}) collective-permute-start(bf16[1,1,1,1,1,8,2048]{6,5,4,3,2,1,0:T(8,128)(2,1)S(1)} %get-tuple-element.117), channel_id=1, source_target_pairs={{0,32},{2,34},{4,36},{6,38},{8,40},{10,42},{12,44},{14,46},{16,48}... | collective-permute-start | bytes 98312 | tf_op jit(solution)/shard_map/ppermute | solution.py:72
  142.2 8.2 %collective-permute-start.30 = (bf16[1,1,1,1,1,8,2048]{6,5,4,3,2,1,0:T(8,128)(2,1)S(1)}, bf16[1,1,1,1,1,8,2048]{6,5,4,3,2,1,0:T(8,128)(2,1)S(1)}, u32[]{:S(2)}, u32[]{:S(2)}) collective-permute-start(bf16[1,1,1,1,1,8,2048]{6,5,4,3,2,1,0:T(8,128)(2,1)S(1)} %get-tuple-element.118), channel_id=1, source_target_pairs={{0,32},{2,34},{4,36},{6,38},{8,40},{10,42},{12,44},{14,46},{16,48}... | collective-permute-start | bytes 98312 | tf_op jit(solution)/shard_map/ppermute | solution.py:72
  150.6 8.3 %collective-permute-start.31 = (bf16[2,1,1,1,1,8,2048]{6,5,4,3,2,1,0:T(8,128)(2,1)S(1)}, bf16[2,1,1,1,1,8,2048]{6,5,4,3,2,1,0:T(8,128)(2,1)S(1)}, u32[]{:S(2)}, u32[]{:S(2)}) collective-permute-start(bf16[2,1,1,1,1,8,2048]{6,5,4,3,2,1,0:T(8,128)(2,1)S(1)} %pad_maximum_fusion.23), channel_id=1, source_target_pairs={{0,2},{2,0},{4,6},{6,4},{8,10},{10,8},{12,14},{14,12},{16,18},{18,... | collective-permute-start | bytes 196616 | tf_op jit(solution)/shard_map/ppermute | solution.py:72
  165.1 9.0 %collective-permute-start.33 = (bf16[2,2,1,1,2,8,2048]{6,5,4,3,2,1,0:T(8,128)(2,1)S(1)}, bf16[2,2,1,1,2,8,2048]{6,5,4,3,2,1,0:T(8,128)(2,1)S(1)}, u32[]{:S(2)}, u32[]{:S(2)}) collective-permute-start(bf16[2,2,1,1,2,8,2048]{6,5,4,3,2,1,0:T(8,128)(2,1)S(1)} %pad_maximum_fusion.14), channel_id=1, source_target_pairs={{0,6},{2,4},{4,2},{6,0},{8,14},{10,12},{12,10},{14,8},{16,22},{18,... | collective-permute-start | bytes 786440 | tf_op jit(solution)/shard_map/ppermute | solution.py:72
  170.8 10.5 %collective-permute-start.29 = (bf16[2,2,2,1,2,8,2048]{6,5,4,3,2,1,0:T(8,128)(2,1)S(1)}, bf16[2,2,2,1,2,8,2048]{6,5,4,3,2,1,0:T(8,128)(2,1)S(1)}, u32[]{:S(2)}, u32[]{:S(2)}) collective-permute-start(bf16[2,2,2,1,2,8,2048]{6,5,4,3,2,1,0:T(8,128)(2,1)S(1)} %pad_maximum_fusion.9), channel_id=1, source_target_pairs={{0,6},{2,4},{4,2},{6,0},{8,14},{10,12},{12,10},{14,8},{16,22},{18,... | collective-permute-start | bytes 1572872 | tf_op jit(solution)/shard_map/ppermute | solution.py:72
  174.2 9.3 %collective-permute-start.34 = (bf16[2,2,1,2,2,8,2048]{6,5,4,3,2,1,0:T(8,128)(2,1)S(1)}, bf16[2,2,1,2,2,8,2048]{6,5,4,3,2,1,0:T(8,128)(2,1)S(1)}, u32[]{:S(2)}, u32[]{:S(2)}) collective-permute-start(bf16[2,2,1,2,2,8,2048]{6,5,4,3,2,1,0:T(8,128)(2,1)S(1)} %pad_maximum_fusion.10), channel_id=1, source_target_pairs={{0,8},{2,10},{4,12},{6,14},{8,0},{10,2},{12,4},{14,6},{16,24},{18,... | collective-permute-start | bytes 1572872 | tf_op jit(solution)/shard_map/ppermute | solution.py:72
  (34 other events, 195.0 us)
Sparse Core Ops, SparseCore 0:
  185.4 84.0 all-gather.1

commit v3 on v0

--- a/solution.py
+++ b/solution.py
@@ -21,8 +21,14 @@
     return jnp.dot(hidden, w_down, preferred_element_type=jnp.float32)
 
 
-def vocab_terms(token_rows, head_rows, targets, vocab):
-    logits = jnp.einsum("td,vd->tv", token_rows, head_rows, preferred_element_type=jnp.float32)
+def vocab_terms(token_parts, head_rows, targets, vocab):
+    width = token_parts[0].shape[1]
+    logits = sum(
+        jnp.einsum(
+            "td,vd->tv", part, head_rows[:, k * width : (k + 1) * width], preferred_element_type=jnp.float32
+        )
+        for k, part in enumerate(token_parts)
+    )
     peak = jnp.max(logits, axis=1)
     total = jnp.sum(jnp.exp(logits - peak[:, None]), axis=1)
     target = jnp.sum(jnp.where(targets[:, None] == vocab[None, :], logits, 0.0), axis=1)
@@ -53,7 +59,7 @@
     return 3 if bit == 2 else bit
 
 
-def gather_doubling(block, orders=((16, 8, 1, 4, 2), (16, 1, 8, 2, 4))):
+def gather_doubling(block, orders=((16, 8, 1, 4, 2), (16, 1, 8, 2, 4)), joined=True):
     bits = zx_bits()
     spot = lax.axis_index("zx")
     size = lax.axis_size("zx")
@@ -75,7 +81,7 @@
                 [jnp.where(low, held, other), jnp.where(low, other, held)], axis=dim
             )
     rows = [p.reshape((-1,) + p.shape[len(bits) + 1 :]) for p in parts]
-    return jnp.concatenate(rows, axis=-1)
+    return jnp.concatenate(rows, axis=-1) if joined else rows
 
 
 def scatter_halving(full, orders=((2, 4, 1, 8, 16), (4, 2, 8, 1, 16))):
@@ -159,17 +165,17 @@
     partial = jnp.dot(hidden, down, preferred_element_type=jnp.float32)
     mixed = scatter_halving(partial)
     out = (pair_rows.astype(jnp.float32) + mixed).astype(jnp.bfloat16)
-    final = gather_doubling(rms_rows(out, jnp.where(first, pol_final_gain, ref_final_gain)))
+    final = gather_doubling(rms_rows(out, jnp.where(first, pol_final_gain, ref_final_gain)), joined=False)
     mine_out = lax.dynamic_slice_in_dim(out, core * rows, rows, axis=0)
     sent_out = lax.ppermute(lax.dynamic_slice_in_dim(out, (1 - core) * rows, rows, axis=0), "core", SWAP)
     pol_out = jnp.where(first, mine_out, sent_out)
     ref_out = jnp.where(first, sent_out, mine_out)
 
-    every = lax.all_gather(final, "grp", axis=0, tiled=True)
+    every = [lax.all_gather(part, "grp", axis=0, tiled=True) for part in final]
     keep_v, give_v = pick(first, pol_head, ref_head)
     got_v = lax.ppermute(give_v, "core", SWAP)
     voc_dev = pol_head.shape[0]
-    positions = jnp.arange(every.shape[0], dtype=jnp.int32)
+    positions = jnp.arange(every[0].shape[0], dtype=jnp.int32)
     base = group * per_group
     vocab = jnp.concatenate(
         [

time: 322 us -> 344 us (1.068); the launches traced: 322 us -> 337 us
  starting transfers between devices: 55.5 us -> 62.3 us
  matrix products: 14 us -> 18.5 us
    ppermute x20, waiting for transfers between devices: 62.5 us -> 81.1 us  [gather_doubling(): lax.ppermute(held, 'zx', [(i, i ^ partner_mask(bit)) for i in range(size)])]
    all_gather x1 -> x2, waiting for transfers between devices: 74.4 us -> 60 us  [per_device(): every = [lax.all_gather(part, 'grp', axis=0, tiled=True) for part in final]]
    ppermute x20, starting transfers between devices: 30.3 us -> 34.9 us  [gather_doubling(): lax.ppermute(held, 'zx', [(i, i ^ partner_mask(bit)) for i in range(size)])]
    dot_general x1 -> x2, matrix products: 7.62 us -> 12.1 us  [vocab_terms(): jnp.einsum('td,vd->tv', part, head_rows[:, k * width:(k + 1) * width], pr...]
    ppermute x10, starting transfers between devices: 8.42 us -> 11.9 us  [scatter_halving(): lax.ppermute(jnp.where(low, upper, lower), 'zx', [(i, i ^ partner_mask(bi...]
  transfers between devices with their start and end apart: 45 -> 46, of which waited for: 36 -> 41; matrix products, arithmetic and copies ran while one was open for 6% -> 7% of each run, Pallas kernels for 0% -> 0%
where the time goes in v3:
time: 344 us; the launch traced here: 337 us
  waiting for transfers between devices  217 us (63%)
  starting transfers between devices  62.3 us (18%)
  matrix products  18.5 us (5%)
  other arithmetic  16.3 us (5%)
  between operations  15.3 us (4%)
  local copies, waits for them, and re-layouts  7.03 us (2%)
    ppermute x20, waiting for transfers between devices, gather_doubling(): lax.ppermute(held, 'zx', [(i, i ^ partner_mask(bit)) for i in range(size)])  81.1 us
    all_gather x2, waiting for transfers between devices, per_device(): every = [lax.all_gather(part, 'grp', axis=0, tiled=True) for part in final]  60 us
    ppermute x10, waiting for transfers between devices, scatter_halving(): lax.ppermute(jnp.where(low, upper, lower), 'zx', [(i, i ^ partner_mask(bi...  51 us
    ppermute x20, starting transfers between devices, gather_doubling(): lax.ppermute(held, 'zx', [(i, i ^ partner_mask(bit)) for i in range(size)])  34.9 us
    ppermute x7, waiting for transfers between devices, per_device(): lax.ppermute(state, axis, [(i, i ^ partner_mask(bit)) for i in range(size)])  19.7 us
    ppermute x7, starting transfers between devices, per_device(): lax.ppermute(state, axis, [(i, i ^ partner_mask(bit)) for i in range(size)])  14 us
    dot_general x2, matrix products, vocab_terms(): jnp.einsum('td,vd->tv', part, head_rows[:, k * width:(k + 1) * width], pr...  12.1 us
    ppermute x10, starting transfers between devices, scatter_halving(): lax.ppermute(jnp.where(low, upper, lower), 'zx', [(i, i ^ partner_mask(bi...  11.9 us
  transfers between devices with their start and end apart: 46, of which 41 were waited for; matrix products, arithmetic and copies ran while one was open for 7% of the time, Pallas kernels for 0%

profile of v3, /device:TPU:6, one launch (start us, length us, event | category | flops | bytes accessed | tf_op | source)
XLA Modules:
  0.0 336.8 jit_solution(13767745429062780843)
XLA Ops:
  7.2 4.3 %conditional.1 = (bf16[172,4096]{1,0:T(8,128)(2,1)S(1)}, bf16[4096,172]{0,1:T(8,128)(2,1)}, bf16[4096,172]{0,1:T(8,128)(2,1)}) conditional(s32[]{:T(128)} %convert_element_type.38, (bf16[4096,172]{0,1:T(8,128)(2,1)}, bf16[4096,172]{0,1:T(8,128)(2,1)}, bf16[172,4096]{1,0:T(8,128)(2,1)}) %tuple.14, (bf16[4096,172]{0,1:T(8,128)(2,1)}, ...), branch_computations={%region_1.0_spmd, %region_2.3_spmd} | conditional | bytes 19726416 | solution.py:147
  17.0 7.3 %collective-permute-start.1 = (bf16[1,1,1,1,1,8,2048]{6,5,4,3,2,1,0:T(8,128)(2,1)S(1)}, bf16[1,1,1,1,1,8,2048]{6,5,4,3,2,1,0:T(8,128)(2,1)S(1)}, u32[]{:S(2)}, u32[]{:S(2)}) collective-permute-start(bf16[1,1,1,1,1,8,2048]{6,5,4,3,2,1,0:T(8,128)(2,1)S(1)} %get-tuple-element.115), channel_id=1, source_target_pairs={{0,32},{2,34},{4,36},{6,38},{8,40},{10,42},{12,44},{14,46},{16,48}... | collective-permute-start | bytes 98312 | tf_op jit(solution)/shard_map/ppermute | solution.py:78
  26.2 5.9 %collective-permute-done.6 = bf16[1,1,1,1,1,8,2048]{6,5,4,3,2,1,0:T(8,128)(2,1)S(1)} collective-permute-done((bf16[1,1,1,1,1,8,2048]{6,5,4,3,2,1,0:T(8,128)(2,1)S(1)}, bf16[1,1,1,1,1,8,2048]{6,5,4,3,2,1,0:T(8,128)(2,1)S(1)}, u32[]{:S(2)}, u32[]{:S(2)}) %collective-permute-start.6) | collective-permute-done | bytes 32800 | tf_op jit(solution)/shard_map/ppermute | solution.py:78
  41.5 4.8 %collective-permute-done.8 = bf16[2,1,1,1,2,8,2048]{6,5,4,3,2,1,0:T(8,128)(2,1)S(1)} collective-permute-done((bf16[2,1,1,1,2,8,2048]{6,5,4,3,2,1,0:T(8,128)(2,1)S(1)}, bf16[2,1,1,1,2,8,2048]{6,5,4,3,2,1,0:T(8,128)(2,1)S(1)}, u32[]{:S(2)}, u32[]{:S(2)}) %collective-permute-start.8) | collective-permute-done | bytes 131104 | tf_op jit(solution)/shard_map/ppermute | solution.py:78
  47.8 6.9 %collective-permute-done.9 = bf16[2,2,1,1,2,8,2048]{6,5,4,3,2,1,0:T(8,128)(2,1)S(1)} collective-permute-done((bf16[2,2,1,1,2,8,2048]{6,5,4,3,2,1,0:T(8,128)(2,1)S(1)}, bf16[2,2,1,1,2,8,2048]{6,5,4,3,2,1,0:T(8,128)(2,1)S(1)}, u32[]{:S(2)}, u32[]{:S(2)}) %collective-permute-start.9) | collective-permute-done | bytes 262176 | tf_op jit(solution)/shard_map/ppermute | solution.py:78
  59.4 6.0 %collective-permute-done.10 = bf16[2,2,1,2,2,8,2048]{6,5,4,3,2,1,0:T(8,128)(2,1)S(1)} collective-permute-done((bf16[2,2,1,2,2,8,2048]{6,5,4,3,2,1,0:T(8,128)(2,1)S(1)}, bf16[2,2,1,2,2,8,2048]{6,5,4,3,2,1,0:T(8,128)(2,1)S(1)}, u32[]{:S(2)}, u32[]{:S(2)}) %collective-permute-start.10) | collective-permute-done | bytes 524320 | tf_op jit(solution)/shard_map/ppermute | solution.py:78
  79.0 17.4 %collective-permute-done.19 = f32[2,2,1,2,2,8,2048]{6,5,4,3,2,1,0:T(8,128)S(1)} collective-permute-done((f32[2,2,1,2,2,8,2048]{6,5,4,3,2,1,0:T(8,128)S(1)}, f32[2,2,1,2,2,8,2048]{6,5,4,3,2,1,0:T(8,128)S(1)}, u32[]{:S(2)}, u32[]{:S(2)}) %collective-permute-start.19) | collective-permute-done | bytes 1048608 | tf_op jit(solution)/shard_map/ppermute | solution.py:106
  110.4 6.7 %collective-permute-done.15 = f32[2,2,1,1,2,8,2048]{6,5,4,3,2,1,0:T(8,128)S(1)} collective-permute-done((f32[2,2,1,1,2,8,2048]{6,5,4,3,2,1,0:T(8,128)S(1)}, f32[2,2,1,1,2,8,2048]{6,5,4,3,2,1,0:T(8,128)S(1)}, u32[]{:S(2)}, u32[]{:S(2)}) %collective-permute-start.15) | collective-permute-done | bytes 524320 | tf_op jit(solution)/shard_map/ppermute | solution.py:106
  126.2 5.5 %collective-permute-done.17 = f32[2,1,1,1,1,8,2048]{6,5,4,3,2,1,0:T(8,128)S(1)} collective-permute-done((f32[2,1,1,1,1,8,2048]{6,5,4,3,2,1,0:T(8,128)S(1)}, f32[2,1,1,1,1,8,2048]{6,5,4,3,2,1,0:T(8,128)S(1)}, u32[]{:S(2)}, u32[]{:S(2)}) %collective-permute-start.17) | collective-permute-done | bytes 131104 | tf_op jit(solution)/shard_map/ppermute | solution.py:106
  134.4 6.0 %collective-permute-done.18 = f32[1,1,1,1,1,8,2048]{6,5,4,3,2,1,0:T(8,128)S(1)} collective-permute-done((f32[1,1,1,1,1,8,2048]{6,5,4,3,2,1,0:T(8,128)S(1)}, f32[1,1,1,1,1,8,2048]{6,5,4,3,2,1,0:T(8,128)S(1)}, u32[]{:S(2)}, u32[]{:S(2)}) %collective-permute-start.18) | collective-permute-done | bytes 65568 | tf_op jit(solution)/shard_map/ppermute | solution.py:106
  141.1 5.8 %collective-permute-start.31 = (bf16[1,1,1,1,1,8,2048]{6,5,4,3,2,1,0:T(8,128)(2,1)S(1)}, bf16[1,1,1,1,1,8,2048]{6,5,4,3,2,1,0:T(8,128)(2,1)S(1)}, u32[]{:S(2)}, u32[]{:S(2)}) collective-permute-start(bf16[1,1,1,1,1,8,2048]{6,5,4,3,2,1,0:T(8,128)(2,1)S(1)} %get-tuple-element.112), channel_id=1, source_target_pairs={{0,32},{2,34},{4,36},{6,38},{8,40},{10,42},{12,44},{14,46},{16,48}... | collective-permute-start | bytes 98312 | tf_op jit(solution)/shard_map/ppermute | solution.py:78
  154.2 6.9 %collective-permute-done.33 = bf16[2,1,1,1,2,8,2048]{6,5,4,3,2,1,0:T(8,128)(2,1)S(1)} collective-permute-done((bf16[2,1,1,1,2,8,2048]{6,5,4,3,2,1,0:T(8,128)(2,1)S(1)}, bf16[2,1,1,1,2,8,2048]{6,5,4,3,2,1,0:T(8,128)(2,1)S(1)}, u32[]{:S(2)}, u32[]{:S(2)}) %collective-permute-start.33) | collective-permute-done | bytes 131104 | tf_op jit(solution)/shard_map/ppermute | solution.py:78
  164.4 4.4 %collective-permute-done.34 = bf16[2,2,1,1,2,8,2048]{6,5,4,3,2,1,0:T(8,128)(2,1)S(1)} collective-permute-done((bf16[2,2,1,1,2,8,2048]{6,5,4,3,2,1,0:T(8,128)(2,1)S(1)}, bf16[2,2,1,1,2,8,2048]{6,5,4,3,2,1,0:T(8,128)(2,1)S(1)}, u32[]{:S(2)}, u32[]{:S(2)}) %collective-permute-start.34) | collective-permute-done | bytes 262176 | tf_op jit(solution)/shard_map/ppermute | solution.py:78
  169.2 9.2 %collective-permute-done.35 = bf16[2,2,1,2,2,8,2048]{6,5,4,3,2,1,0:T(8,128)(2,1)S(1)} collective-permute-done((bf16[2,2,1,2,2,8,2048]{6,5,4,3,2,1,0:T(8,128)(2,1)S(1)}, bf16[2,2,1,2,2,8,2048]{6,5,4,3,2,1,0:T(8,128)(2,1)S(1)}, u32[]{:S(2)}, u32[]{:S(2)}) %collective-permute-start.35) | collective-permute-done | bytes 524320 | tf_op jit(solution)/shard_map/ppermute | solution.py:78
  185.2 5.0 %collective-permute-done.27 = bf16[2,2,1,1,1,8,2048]{6,5,4,3,2,1,0:T(8,128)(2,1)S(1)} collective-permute-done((bf16[2,2,1,1,1,8,2048]{6,5,4,3,2,1,0:T(8,128)(2,1)S(1)}, bf16[2,2,1,1,1,8,2048]{6,5,4,3,2,1,0:T(8,128)(2,1)S(1)}, u32[]{:S(2)}, u32[]{:S(2)}) %collective-permute-start.27) | collective-permute-done | bytes 131104 | tf_op jit(solution)/shard_map/ppermute | solution.py:78
  190.3 6.4 %collective-permute-done.28 = bf16[2,2,1,1,2,8,2048]{6,5,4,3,2,1,0:T(8,128)(2,1)S(1)} collective-permute-done((bf16[2,2,1,1,2,8,2048]{6,5,4,3,2,1,0:T(8,128)(2,1)S(1)}, bf16[2,2,1,1,2,8,2048]{6,5,4,3,2,1,0:T(8,128)(2,1)S(1)}, u32[]{:S(2)}, u32[]{:S(2)}) %collective-permute-start.28) | collective-permute-done | bytes 262176 | tf_op jit(solution)/shard_map/ppermute | solution.py:78
  196.8 5.0 %collective-permute-start.29 = (bf16[2,2,2,1,2,8,2048]{6,5,4,3,2,1,0:T(8,128)(2,1)S(1)}, bf16[2,2,2,1,2,8,2048]{6,5,4,3,2,1,0:T(8,128)(2,1)S(1)}, u32[]{:S(2)}, u32[]{:S(2)}) collective-permute-start(bf16[2,2,2,1,2,8,2048]{6,5,4,3,2,1,0:T(8,128)(2,1)S(1)} %pad_maximum_fusion.10), channel_id=1, source_target_pairs={{0,6},{2,4},{4,2},{6,0},{8,14},{10,12},{12,10},{14,8},{16,22},{18,... | collective-permute-start | bytes 1572872 | tf_op jit(solution)/shard_map/ppermute | solution.py:78
  201.7 7.2 %collective-permute-done.29 = bf16[2,2,2,1,2,8,2048]{6,5,4,3,2,1,0:T(8,128)(2,1)S(1)} collective-permute-done((bf16[2,2,2,1,2,8,2048]{6,5,4,3,2,1,0:T(8,128)(2,1)S(1)}, bf16[2,2,2,1,2,8,2048]{6,5,4,3,2,1,0:T(8,128)(2,1)S(1)}, u32[]{:S(2)}, u32[]{:S(2)}) %collective-permute-start.29) | collective-permute-done | bytes 524320 | tf_op jit(solution)/shard_map/ppermute | solution.py:78
  219.4 13.6 %all-gather.5.cloned.1.call-done = bf16[1024,2048]{1,0:T(8,128)(2,1)} async-done(((bf16[256,2048]{1,0:T(8,128)(2,1)}), bf16[1024,2048]{1,0:T(8,128)(2,1)}) %all-gather.5.cloned.1.call-update) | async-done | bytes 4194320 | tf_op jit(solution)/shard_map/all_gather | solution.py:174
  232.9 6.6 %fusion.21 = f32[1024,500]{0,1:T(8,128)} fusion(bf16[1024,2048]{1,0:T(8,128)(2,1)} %all-gather.5.cloned.1.call-done, bf16[250,4096]{1,0:T(8,128)(2,1)} %copy-done.18, bf16[250,4096]{1,0:T(8,128)(2,1)} %get-tuple-element.63), kind=kOutput, calls=%fused_computation.27 | convolution fusion | flops 2101248000 | bytes 10338304 | tf_op jit(solution)/shard_map/td,vd->tv/dot_general | solution.py:27
  239.5 46.4 %all-gather.3.cloned.1.call-done = bf16[1024,2048]{1,0:T(8,128)(2,1)} async-done(((bf16[256,2048]{1,0:T(8,128)(2,1)}), bf16[1024,2048]{1,0:T(8,128)(2,1)}) %all-gather.3.cloned.1.call-update) | async-done | bytes 4194320 | tf_op jit(solution)/shard_map/all_gather | solution.py:174
  286.0 5.5 %fusion.54 = (f32[1024]{0:T(1024)S(1)}, f32[1024,500]{0,1:T(8,128)S(1)}) fusion(f32[1024,500]{0,1:T(8,128)} %fusion.21, bf16[1024,2048]{1,0:T(8,128)(2,1)} %all-gather.3.cloned.1.call-done, bf16[250,4096]{1,0:T(8,128)(2,1)S(1)} %copy-done.7, bf16[250,4096]{1,0:T(8,128)(2,1)} %copy-done.18), kind=kOutput, calls=%fused_computation.219 | convolution fusion | flops 2102270976 | bytes 12390400 | tf_op jit(solution)/shard_map/td,vd->tv/dot_general | solution.py:27
  298.3 4.5 %collective-permute-done.38 = f32[2,3,1024]{2,0,1:T(2,128)S(1)} collective-permute-done((f32[2,3,1024]{2,0,1:T(2,128)S(1)}, f32[2,3,1024]{2,0,1:T(2,128)S(1)}, u32[]{:S(2)}, u32[]{:S(2)}) %collective-permute-start.38) | collective-permute-done | bytes 24608 | tf_op jit(solution)/shard_map/ppermute | solution.py:192
  311.8 5.8 %collective-permute-start.41 = (f32[2,3,1024]{2,0,1:T(2,128)S(1)}, f32[2,3,1024]{2,0,1:T(2,128)S(1)}, u32[]{:S(2)}, u32[]{:S(2)}) collective-permute-start(f32[2,3,1024]{2,0,1:T(2,128)S(1)} %pad_maximum_fusion.27), channel_id=1, source_target_pairs={{0,32},{2,34},{4,36},{6,38},{8,40},{10,42},{12,44},{14,46},{16,48}... | collective-permute-start | bytes 73736 | tf_op jit(solution)/shard_map/ppermute | solution.py:192
  (221 shorter events, 122.6 us)
Async XLA Ops:
  7.2 225.8 %all-gather.5.cloned.1.call-start = ((), (), s32[]{:S(2)}) async-start(), calls=%async_computation.1 | async-start | bytes 5242880 | tf_op jit(solution)/shard_map/all_gather | solution.py:174
  11.6 61.3 %collective-permute-start.13 = (bf16[172,4096]{1,0:T(8,128)(2,1)S(1)}, bf16[172,4096]{1,0:T(8,128)(2,1)}, u32[]{:S(2)}, u32[]{:S(2)}) collective-permute-start(bf16[172,4096]{1,0:T(8,128)(2,1)S(1)} %get-tuple-element.20), channel_id=1, source_target_pairs={{0,1},{1,0},{2,3},{3,2},{4,5},{5,4},{6,7},{7,6},{8,9},{9,8},{10,11... | collective-permute-start | bytes 4227080 | tf_op jit(solution)/shard_map/ppermute | solution.py:147
  11.6 56.5 %collective-permute-start.12 = (bf16[4096,172]{0,1:T(8,128)(2,1)}, bf16[4096,172]{0,1:T(8,128)(2,1)}, u32[]{:S(2)}, u32[]{:S(2)}) collective-permute-start(bf16[4096,172]{0,1:T(8,128)(2,1)} %get-tuple-element.46), channel_id=1, source_target_pairs={{0,1},{1,0},{2,3},{3,2},{4,5},{5,4},{6,7},{7,6},{8,9},{9,8},{10,11... | collective-permute-start | bytes 4227080 | tf_op jit(solution)/shard_map/ppermute | solution.py:147
  12.1 56.0 %collective-permute-start.11 = (bf16[4096,172]{0,1:T(8,128)(2,1)}, bf16[4096,172]{0,1:T(8,128)(2,1)}, u32[]{:S(2)}, u32[]{:S(2)}) collective-permute-start(bf16[4096,172]{0,1:T(8,128)(2,1)} %get-tuple-element.45), channel_id=1, source_target_pairs={{0,1},{1,0},{2,3},{3,2},{4,5},{5,4},{6,7},{7,6},{8,9},{9,8},{10,11... | collective-permute-start | bytes 4227080 | tf_op jit(solution)/shard_map/ppermute | solution.py:147
  17.0 9.2 %collective-permute-start.1 = (bf16[1,1,1,1,1,8,2048]{6,5,4,3,2,1,0:T(8,128)(2,1)S(1)}, bf16[1,1,1,1,1,8,2048]{6,5,4,3,2,1,0:T(8,128)(2,1)S(1)}, u32[]{:S(2)}, u32[]{:S(2)}) collective-permute-start(bf16[1,1,1,1,1,8,2048]{6,5,4,3,2,1,0:T(8,128)(2,1)S(1)} %get-tuple-element.115), channel_id=1, source_target_pairs={{0,32},{2,34},{4,36},{6,38},{8,40},{10,42},{12,44},{14,46},{16,48}... | collective-permute-start | bytes 98312 | tf_op jit(solution)/shard_map/ppermute | solution.py:78
  24.3 7.8 %collective-permute-start.6 = (bf16[1,1,1,1,1,8,2048]{6,5,4,3,2,1,0:T(8,128)(2,1)S(1)}, bf16[1,1,1,1,1,8,2048]{6,5,4,3,2,1,0:T(8,128)(2,1)S(1)}, u32[]{:S(2)}, u32[]{:S(2)}) collective-permute-start(bf16[1,1,1,1,1,8,2048]{6,5,4,3,2,1,0:T(8,128)(2,1)S(1)} %get-tuple-element.116), channel_id=1, source_target_pairs={{0,32},{2,34},{4,36},{6,38},{8,40},{10,42},{12,44},{14,46},{16,48}... | collective-permute-start | bytes 98312 | tf_op jit(solution)/shard_map/ppermute | solution.py:78
  46.4 8.3 %collective-permute-start.9 = (bf16[2,2,1,1,2,8,2048]{6,5,4,3,2,1,0:T(8,128)(2,1)S(1)}, bf16[2,2,1,1,2,8,2048]{6,5,4,3,2,1,0:T(8,128)(2,1)S(1)}, u32[]{:S(2)}, u32[]{:S(2)}) collective-permute-start(bf16[2,2,1,1,2,8,2048]{6,5,4,3,2,1,0:T(8,128)(2,1)S(1)} %pad_maximum_fusion.13), channel_id=1, source_target_pairs={{0,6},{2,4},{4,2},{6,0},{8,14},{10,12},{12,10},{14,8},{16,22},{18,... | collective-permute-start | bytes 786440 | tf_op jit(solution)/shard_map/ppermute | solution.py:78
  47.7 8.9 %collective-permute-start.4 = (bf16[2,2,1,1,2,8,2048]{6,5,4,3,2,1,0:T(8,128)(2,1)S(1)}, bf16[2,2,1,1,2,8,2048]{6,5,4,3,2,1,0:T(8,128)(2,1)S(1)}, u32[]{:S(2)}, u32[]{:S(2)}) collective-permute-start(bf16[2,2,1,1,2,8,2048]{6,5,4,3,2,1,0:T(8,128)(2,1)S(1)} %pad_maximum_fusion.12), channel_id=1, source_target_pairs={{0,8},{2,10},{4,12},{6,14},{8,0},{10,2},{12,4},{14,6},{16,24},{18,... | collective-permute-start | bytes 786440 | tf_op jit(solution)/shard_map/ppermute | solution.py:78
  54.8 10.5 %collective-permute-start.10 = (bf16[2,2,1,2,2,8,2048]{6,5,4,3,2,1,0:T(8,128)(2,1)S(1)}, bf16[2,2,1,2,2,8,2048]{6,5,4,3,2,1,0:T(8,128)(2,1)S(1)}, u32[]{:S(2)}, u32[]{:S(2)}) collective-permute-start(bf16[2,2,1,2,2,8,2048]{6,5,4,3,2,1,0:T(8,128)(2,1)S(1)} %pad_maximum_fusion.9), channel_id=1, source_target_pairs={{0,8},{2,10},{4,12},{6,14},{8,0},{10,2},{12,4},{14,6},{16,24},{18,... | collective-permute-start | bytes 1572872 | tf_op jit(solution)/shard_map/ppermute | solution.py:78
  56.7 10.7 %collective-permute-start.5 = (bf16[2,2,2,1,2,8,2048]{6,5,4,3,2,1,0:T(8,128)(2,1)S(1)}, bf16[2,2,2,1,2,8,2048]{6,5,4,3,2,1,0:T(8,128)(2,1)S(1)}, u32[]{:S(2)}, u32[]{:S(2)}) collective-permute-start(bf16[2,2,2,1,2,8,2048]{6,5,4,3,2,1,0:T(8,128)(2,1)S(1)} %pad_maximum_fusion.8), channel_id=1, source_target_pairs={{0,6},{2,4},{4,2},{6,0},{8,14},{10,12},{12,10},{14,8},{16,22},{18,... | collective-permute-start | bytes 1572872 | tf_op jit(solution)/shard_map/ppermute | solution.py:78
  76.3 20.2 %collective-permute-start.19 = (f32[2,2,1,2,2,8,2048]{6,5,4,3,2,1,0:T(8,128)S(1)}, f32[2,2,1,2,2,8,2048]{6,5,4,3,2,1,0:T(8,128)S(1)}, u32[]{:S(2)}, u32[]{:S(2)}) collective-permute-start(f32[2,2,1,2,2,8,2048]{6,5,4,3,2,1,0:T(8,128)S(1)} %slice_select_fusion), channel_id=1, source_target_pairs={{0,8},{2,10},{4,12},{6,14},{8,0},{10,2},{12,4},{14,6},{16,24},{18,... | collective-permute-start | bytes 3145736 | tf_op jit(solution)/shard_map/ppermute | solution.py:106
  76.8 24.1 %collective-permute-start.14 = (f32[2,2,2,1,2,8,2048]{6,5,4,3,2,1,0:T(8,128)S(1)}, f32[2,2,2,1,2,8,2048]{6,5,4,3,2,1,0:T(8,128)S(1)}, u32[]{:S(2)}, u32[]{:S(2)}) collective-permute-start(f32[2,2,2,1,2,8,2048]{6,5,4,3,2,1,0:T(8,128)S(1)} %slice_select_fusion.1), channel_id=1, source_target_pairs={{0,6},{2,4},{4,2},{6,0},{8,14},{10,12},{12,10},{14,8},{16,22},{18,... | collective-permute-start | bytes 3145736 | tf_op jit(solution)/shard_map/ppermute | solution.py:106
  96.7 11.3 %collective-permute-start.20 = (f32[2,2,1,1,2,8,2048]{6,5,4,3,2,1,0:T(8,128)S(1)}, f32[2,2,1,1,2,8,2048]{6,5,4,3,2,1,0:T(8,128)S(1)}, u32[]{:S(2)}, u32[]{:S(2)}) collective-permute-start(f32[2,2,1,1,2,8,2048]{6,5,4,3,2,1,0:T(8,128)S(1)} %slice_select_fusion.2), channel_id=1, source_target_pairs={{0,6},{2,4},{4,2},{6,0},{8,14},{10,12},{12,10},{14,8},{16,22},{18,... | collective-permute-start | bytes 1572872 | tf_op jit(solution)/shard_map/ppermute | solution.py:106
  101.3 15.8 %collective-permute-start.15 = (f32[2,2,1,1,2,8,2048]{6,5,4,3,2,1,0:T(8,128)S(1)}, f32[2,2,1,1,2,8,2048]{6,5,4,3,2,1,0:T(8,128)S(1)}, u32[]{:S(2)}, u32[]{:S(2)}) collective-permute-start(f32[2,2,1,1,2,8,2048]{6,5,4,3,2,1,0:T(8,128)S(1)} %slice_select_fusion.3), channel_id=1, source_target_pairs={{0,8},{2,10},{4,12},{6,14},{8,0},{10,2},{12,4},{14,6},{16,24},{18,... | collective-permute-start | bytes 1572872 | tf_op jit(solution)/shard_map/ppermute | solution.py:106
  108.1 12.8 %collective-permute-start.21 = (f32[2,1,1,1,2,8,2048]{6,5,4,3,2,1,0:T(8,128)S(1)}, f32[2,1,1,1,2,8,2048]{6,5,4,3,2,1,0:T(8,128)S(1)}, u32[]{:S(2)}, u32[]{:S(2)}) collective-permute-start(f32[2,1,1,1,2,8,2048]{6,5,4,3,2,1,0:T(8,128)S(1)} %slice_select_fusion.4), channel_id=1, source_target_pairs={{0,16},{2,18},{4,20},{6,22},{8,24},{10,26},{12,28},{14,30},{16,0},... | collective-permute-start | bytes 786440 | tf_op jit(solution)/shard_map/ppermute | solution.py:106
  123.8 8.0 %collective-permute-start.17 = (f32[2,1,1,1,1,8,2048]{6,5,4,3,2,1,0:T(8,128)S(1)}, f32[2,1,1,1,1,8,2048]{6,5,4,3,2,1,0:T(8,128)S(1)}, u32[]{:S(2)}, u32[]{:S(2)}) collective-permute-start(f32[2,1,1,1,1,8,2048]{6,5,4,3,2,1,0:T(8,128)S(1)} %slice_select_fusion.7), channel_id=1, source_target_pairs={{0,16},{2,18},{4,20},{6,22},{8,24},{10,26},{12,28},{14,30},{16,0},... | collective-permute-start | bytes 393224 | tf_op jit(solution)/shard_map/ppermute | solution.py:106
  126.1 8.3 %collective-permute-start.23 = (f32[1,1,1,1,1,8,2048]{6,5,4,3,2,1,0:T(8,128)S(1)}, f32[1,1,1,1,1,8,2048]{6,5,4,3,2,1,0:T(8,128)S(1)}, u32[]{:S(2)}, u32[]{:S(2)}) collective-permute-start(f32[1,1,1,1,1,8,2048]{6,5,4,3,2,1,0:T(8,128)S(1)} %slice_select_fusion.8), channel_id=1, source_target_pairs={{0,32},{2,34},{4,36},{6,38},{8,40},{10,42},{12,44},{14,46},{16,48}... | collective-permute-start | bytes 196616 | tf_op jit(solution)/shard_map/ppermute | solution.py:106
  131.8 8.6 %collective-permute-start.18 = (f32[1,1,1,1,1,8,2048]{6,5,4,3,2,1,0:T(8,128)S(1)}, f32[1,1,1,1,1,8,2048]{6,5,4,3,2,1,0:T(8,128)S(1)}, u32[]{:S(2)}, u32[]{:S(2)}) collective-permute-start(f32[1,1,1,1,1,8,2048]{6,5,4,3,2,1,0:T(8,128)S(1)} %slice_select_fusion.9), channel_id=1, source_target_pairs={{0,32},{2,34},{4,36},{6,38},{8,40},{10,42},{12,44},{14,46},{16,48}... | collective-permute-start | bytes 196616 | tf_op jit(solution)/shard_map/ppermute | solution.py:106
  140.7 8.1 %collective-permute-start.25 = (bf16[1,1,1,1,1,8,2048]{6,5,4,3,2,1,0:T(8,128)(2,1)S(1)}, bf16[1,1,1,1,1,8,2048]{6,5,4,3,2,1,0:T(8,128)(2,1)S(1)}, u32[]{:S(2)}, u32[]{:S(2)}) collective-permute-start(bf16[1,1,1,1,1,8,2048]{6,5,4,3,2,1,0:T(8,128)(2,1)S(1)} %get-tuple-element.111), channel_id=1, source_target_pairs={{0,32},{2,34},{4,36},{6,38},{8,40},{10,42},{12,44},{14,46},{16,48}... | collective-permute-start | bytes 98312 | tf_op jit(solution)/shard_map/ppermute | solution.py:78
  141.1 8.1 %collective-permute-start.31 = (bf16[1,1,1,1,1,8,2048]{6,5,4,3,2,1,0:T(8,128)(2,1)S(1)}, bf16[1,1,1,1,1,8,2048]{6,5,4,3,2,1,0:T(8,128)(2,1)S(1)}, u32[]{:S(2)}, u32[]{:S(2)}) collective-permute-start(bf16[1,1,1,1,1,8,2048]{6,5,4,3,2,1,0:T(8,128)(2,1)S(1)} %get-tuple-element.112), channel_id=1, source_target_pairs={{0,32},{2,34},{4,36},{6,38},{8,40},{10,42},{12,44},{14,46},{16,48}... | collective-permute-start | bytes 98312 | tf_op jit(solution)/shard_map/ppermute | solution.py:78
  168.9 9.5 %collective-permute-start.35 = (bf16[2,2,1,2,2,8,2048]{6,5,4,3,2,1,0:T(8,128)(2,1)S(1)}, bf16[2,2,1,2,2,8,2048]{6,5,4,3,2,1,0:T(8,128)(2,1)S(1)}, u32[]{:S(2)}, u32[]{:S(2)}) collective-permute-start(bf16[2,2,1,2,2,8,2048]{6,5,4,3,2,1,0:T(8,128)(2,1)S(1)} %pad_maximum_fusion.11), channel_id=1, source_target_pairs={{0,8},{2,10},{4,12},{6,14},{8,0},{10,2},{12,4},{14,6},{16,24},{18,... | collective-permute-start | bytes 1572872 | tf_op jit(solution)/shard_map/ppermute | solution.py:78
  179.5 106.4 %all-gather.3.cloned.1.call-start = ((), (), s32[]{:S(2)}) async-start(), calls=%async_computation | async-start | bytes 5242880 | tf_op jit(solution)/shard_map/all_gather | solution.py:174
  196.8 12.1 %collective-permute-start.29 = (bf16[2,2,2,1,2,8,2048]{6,5,4,3,2,1,0:T(8,128)(2,1)S(1)}, bf16[2,2,2,1,2,8,2048]{6,5,4,3,2,1,0:T(8,128)(2,1)S(1)}, u32[]{:S(2)}, u32[]{:S(2)}) collective-permute-start(bf16[2,2,2,1,2,8,2048]{6,5,4,3,2,1,0:T(8,128)(2,1)S(1)} %pad_maximum_fusion.10), channel_id=1, source_target_pairs={{0,6},{2,4},{4,2},{6,0},{8,14},{10,12},{12,10},{14,8},{16,22},{18,... | collective-permute-start | bytes 1572872 | tf_op jit(solution)/shard_map/ppermute | solution.py:78
  311.8 7.8 %collective-permute-start.41 = (f32[2,3,1024]{2,0,1:T(2,128)S(1)}, f32[2,3,1024]{2,0,1:T(2,128)S(1)}, u32[]{:S(2)}, u32[]{:S(2)}) collective-permute-start(f32[2,3,1024]{2,0,1:T(2,128)S(1)} %pad_maximum_fusion.27), channel_id=1, source_target_pairs={{0,32},{2,34},{4,36},{6,38},{8,40},{10,42},{12,44},{14,46},{16,48}... | collective-permute-start | bytes 73736 | tf_op jit(solution)/shard_map/ppermute | solution.py:192
  (39 other events, 320.7 us)
Sparse Core Ops, SparseCore 0:
  179.7 53.2 all-gather.4
  234.7 51.1 all-gather.2
